TPU v7x, 256 devices: a whole 4x4x8 slice. The times are simulated.
256 devices in a mesh: wide: 64 (over z, x, y_lo), narrow: 4 (over y_hi, core).
Axes of the slice: x: 4, y: 4 (y_hi: 2, y_lo: 2; y = y_hi * 2 + y_lo), z: 8, core: 2. Of those that a mesh axis runs over, the one named last changes fastest.
Arguments:
- density: bfloat16 [8192, 8, 128], P(('wide', 'narrow')), may hold values from -6 to 6
- basis: bfloat16 [8192, 64, 128], P(('wide', 'narrow')), may hold values from -0.5 to 0.5
- near_list: int32 [8192, 6], P(('wide', 'narrow')), may hold values from 0 to 8191, as said below
- near_blocks: bfloat16 [8192, 6, 128, 128], P(('wide', 'narrow')), may hold values from -0.21875 to 0.21875
- far_leaf: int32 [8192, 6], P(('wide', 'narrow')), may hold values from 0 to 8191, as said below
- leaf_coupling: bfloat16 [8192, 64, 384], P(('wide', 'narrow')), may hold values from -0.3125 to 0.3125
- transfer: bfloat16 [1024, 64, 512], P(('wide', 'narrow')), may hold values from -0.75 to 0.75
- far_coarse: int32 [1024, 8], P(('wide', 'narrow')), may hold values from 0 to 1023
- coarse_coupling: bfloat16 [1024, 64, 512], P(('wide', 'narrow')), may hold values from -0.25 to 0.25
Outputs:
- potential: bfloat16 [8192, 8, 128], P(('wide', 'narrow'))
Inputs may be any that keep to these rules, and one draw needn't show every extreme that they name: `near_list`: every entry lies within 32 leaves of its own leaf l; the first entry is l itself. `far_leaf`: every entry lies within 32 leaves of its own leaf.
All inputs are finite; a program needn't handle non-finite values.
Results may differ from a plain program's by a relative error of at most 0.0066.
Values may be sent and summed in bfloat16 or wider, within the bound.
No kernel may reach another device: no remote copies, remote signals or barrier semaphores. Data moves between devices by JAX's collectives and lax.ppermute only.
A program may use at most 64 MiB of HBM per device.

v0:
```python
import jax
import jax.numpy as jnp
from jax import lax
from jax.sharding import PartitionSpec as P


def with_halo(block, sides, width):
    for axis, dim in sides:
        count = lax.axis_size(axis)
        forward = [(i, i + 1) for i in range(count - 1)]
        backward = [(target, source) for source, target in forward]
        low = lax.ppermute(
            lax.slice_in_dim(block, block.shape[dim] - width, None, axis=dim), axis, forward
        )
        high = lax.ppermute(lax.slice_in_dim(block, 0, width, axis=dim), axis, backward)
        block = jnp.concatenate([low, block, high], axis=dim)
    return block


def body(
    density,
    basis,
    near_list,
    near_blocks,
    far_leaf,
    leaf_coupling,
    transfer,
    far_coarse,
    coarse_coupling,
):
    leaf_count, rhs_count, leaf_width = density.shape
    rank_width = basis.shape[1]
    box_count = transfer.shape[0]
    child_count = leaf_count // box_count
    far_count = far_leaf.shape[1]
    coarse_count = far_coarse.shape[1]
    skeleton = jnp.einsum(
        "lrp,lkp->lrk", density, basis, preferred_element_type=jnp.float32
    ).astype(jnp.bfloat16)
    children = skeleton.reshape(box_count, child_count, rhs_count, rank_width)
    coarse = jnp.einsum(
        "ckim,cirm->crk",
        transfer.reshape(box_count, rank_width, child_count, rank_width),
        children,
        preferred_element_type=jnp.float32,
    ).astype(jnp.bfloat16)
    coarse_flat = coarse.reshape(box_count, rhs_count * rank_width)
    everything = lax.all_gather(coarse_flat, ("wide", "narrow"), axis=0, tiled=True)
    offset_base = lax.axis_index(("wide", "narrow")) * leaf_count - leaf_count
    density_flat = density.reshape(leaf_count, rhs_count * leaf_width)
    skeleton_flat = skeleton.reshape(leaf_count, rhs_count * rank_width)
    density_padded = with_halo(density_flat, ((("wide", "narrow"), 0),), leaf_count)
    skeleton_padded = with_halo(skeleton_flat, ((("wide", "narrow"), 0),), leaf_count)
    near_rows = jnp.take(density_padded, near_list - offset_base, axis=0).reshape(
        leaf_count, near_list.shape[1], rhs_count, leaf_width
    )
    near_part = jnp.einsum(
        "ljpq,ljrq->lrp", near_blocks, near_rows, preferred_element_type=jnp.float32
    )
    far_skels = jnp.take(skeleton_padded, far_leaf - offset_base, axis=0).reshape(
        leaf_count, far_count, rhs_count, rank_width
    )
    leaf_far = jnp.einsum(
        "lkjm,ljrm->lrk",
        leaf_coupling.reshape(leaf_count, rank_width, far_count, rank_width),
        far_skels,
        preferred_element_type=jnp.float32,
    )
    coarse_skels = jnp.take(everything, far_coarse, axis=0).reshape(
        box_count, coarse_count, rhs_count, rank_width
    )
    coarse_field = jnp.einsum(
        "ckjm,cjrm->crk",
        coarse_coupling.reshape(box_count, rank_width, coarse_count, rank_width),
        coarse_skels,
        preferred_element_type=jnp.float32,
    ).astype(jnp.bfloat16)
    descended = jnp.einsum(
        "ckim,crk->cirm",
        transfer.reshape(box_count, rank_width, child_count, rank_width),
        coarse_field,
        preferred_element_type=jnp.float32,
    ).reshape(leaf_count, rhs_count, rank_width)
    local_field = (leaf_far + descended).astype(jnp.bfloat16)
    total = (
        jnp.einsum("lrk,lkp->lrp", local_field, basis, preferred_element_type=jnp.float32)
        + near_part
    )
    return total.astype(jnp.bfloat16)


def solution(mesh):
    return jax.shard_map(
        body,
        mesh=mesh,
        in_specs=(
            P(("wide", "narrow"), None, None),
            P(("wide", "narrow"), None, None),
            P(("wide", "narrow"), None),
            P(("wide", "narrow"), None, None, None),
            P(("wide", "narrow"), None),
            P(("wide", "narrow"), None, None),
            P(("wide", "narrow"), None, None),
            P(("wide", "narrow"), None),
            P(("wide", "narrow"), None, None),
        ),
        out_specs=P(("wide", "narrow"), None, None),
        check_vma=False,
    )
```

profile of v0, /device:TPU:1, one launch (start us, length us, event | category | flops | bytes accessed | tf_op | source)
XLA Modules:
  0.0 415.8 jit_solution(6221959910823239641)
XLA Ops:
  6.5 1.4 reshape.49
  8.0 1.2 convolution_convert_fusion
  9.2 0.3 fusion.16
  9.4 0.7 reshape.87
  10.2 0.1 reshape.46
  10.3 6.2 %collective-permute-start = (bf16[32,512]{1,0:T(8,128)(2,1)S(1)}, bf16[32,512]{1,0:T(8,128)(2,1)S(1)}, u32[]{:S(2)}, u32[]{:S(2)}) collective-permute-start(bf16[32,512]{1,0:T(8,128)(2,1)S(1)} %reshape.46), channel_id=1, source_target_pairs={{0,1},{1,2},{2,3},{3,4},{4,5},{5,6},{6,7},{7,8},{8,9},{9,10},{10,1... | collective-permute-start | bytes 98312 | tf_op jit(solution)/shard_map/ppermute | solution.py:12
  16.5 1.9 collective-permute-start.1
  18.4 0.9 copy.53
  19.3 5.1 %collective-permute-start.2 = (bf16[32,1024]{1,0:T(8,128)(2,1)S(1)}, bf16[32,1024]{1,0:T(8,128)(2,1)S(1)}, u32[]{:S(2)}, u32[]{:S(2)}) collective-permute-start(bf16[32,1024]{1,0:T(8,128)(2,1)S(1)} %bitcast.57), channel_id=1, source_target_pairs={{0,1},{1,2},{2,3},{3,4},{4,5},{5,6},{6,7},{7,8},{8,9},{9,10},{10,1... | collective-permute-start | bytes 196616 | tf_op jit(solution)/shard_map/ppermute | solution.py:12
  24.4 1.9 collective-permute-start.3
  26.4 0.7 compare_and_fusion
  27.3 0.7 compare_select_fusion.2
  28.3 0.7 compare_and_fusion.2
  29.1 1.3 reshape.51
  30.3 3.7 reshape.47
  34.2 1.0 gather_fusion
  35.2 0.2 gather.19
  35.5 1.0 gather_fusion.2
  36.6 361.3 %all-gather.3.cloned.1.call-done = bf16[256,4,512]{2,1,0:T(4,128)(2,1)} async-done(((bf16[1,4,512]{2,1,0:T(4,128)(2,1)}), bf16[256,4,512]{2,1,0:T(4,128)(2,1)}) %all-gather.3.cloned.1.call-update) | async-done | bytes 1048592 | tf_op jit(solution)/shard_map/all_gather | solution.py:48
  397.9 1.3 reshape.88
  399.2 0.6 gather_fusion.1
  399.9 0.4 fusion.19
  400.4 3.4 fusion.14
  403.8 5.2 %fusion.12 = bf16[32,8,128]{2,1,0:T(8,128)(2,1)} fusion(f32[32,8,128]{2,1,0:T(8,128)S(1)} %fusion.14, bf16[32,6,128,128]{3,2,1,0:T(8,128)(2,1)} %param.12, bf16[32,6,8,128]{3,2,1,0:T(8,128)(2,1)S(1)} %bitcast.53, pred[32,6]{1,0:T(8,128)(4,1)S(1)} %copy.26), kind=kOutput, calls=%fused_computation.10 | convolution fusion | flops 50593792 | bytes 6881472 | tf_op jit(solution)/shard_map/ljpq,ljrq->lrp/dot_general | solution.py:57
  (24 shorter events, 0.9 us)
Async XLA Ops:
  6.5 1.4 copy-start
  6.5 23.8 %copy-start.1 = (bf16[32,64,384]{2,1,0:T(8,128)(2,1)S(1)}, bf16[32,64,384]{2,1,0:T(8,128)(2,1)}, u32[]{:S(2)}) copy-start(bf16[32,64,384]{2,1,0:T(8,128)(2,1)} %param.14) | copy-start | bytes 4718596
  6.5 391.3 %all-gather.3.cloned.1.call-start = ((), (), s32[]{:S(2)}) async-start(), calls=%async_computation | async-start | bytes 1052672 | tf_op jit(solution)/shard_map/all_gather | solution.py:48
  10.3 23.9 %collective-permute-start = (bf16[32,512]{1,0:T(8,128)(2,1)S(1)}, bf16[32,512]{1,0:T(8,128)(2,1)S(1)}, u32[]{:S(2)}, u32[]{:S(2)}) collective-permute-start(bf16[32,512]{1,0:T(8,128)(2,1)S(1)} %reshape.46), channel_id=1, source_target_pairs={{0,1},{1,2},{2,3},{3,4},{4,5},{5,6},{6,7},{7,8},{8,9},{9,10},{10,1... | collective-permute-start | bytes 98312 | tf_op jit(solution)/shard_map/ppermute | solution.py:12
  16.5 17.7 %collective-permute-start.1 = (bf16[32,512]{1,0:T(8,128)(2,1)S(1)}, bf16[32,512]{1,0:T(8,128)(2,1)S(1)}, u32[]{:S(2)}, u32[]{:S(2)}) collective-permute-start(bf16[32,512]{1,0:T(8,128)(2,1)S(1)} %reshape.46), channel_id=1, source_target_pairs={{1,0},{2,1},{3,2},{4,3},{5,4},{6,5},{7,6},{8,7},{9,8},{10,9},{11,1... | collective-permute-start | bytes 98312 | tf_op jit(solution)/shard_map/ppermute | solution.py:15
  19.3 16.2 %collective-permute-start.2 = (bf16[32,1024]{1,0:T(8,128)(2,1)S(1)}, bf16[32,1024]{1,0:T(8,128)(2,1)S(1)}, u32[]{:S(2)}, u32[]{:S(2)}) collective-permute-start(bf16[32,1024]{1,0:T(8,128)(2,1)S(1)} %bitcast.57), channel_id=1, source_target_pairs={{0,1},{1,2},{2,3},{3,4},{4,5},{5,6},{6,7},{7,8},{8,9},{9,10},{10,1... | collective-permute-start | bytes 196616 | tf_op jit(solution)/shard_map/ppermute | solution.py:12
  24.4 11.0 %collective-permute-start.3 = (bf16[32,1024]{1,0:T(8,128)(2,1)S(1)}, bf16[32,1024]{1,0:T(8,128)(2,1)S(1)}, u32[]{:S(2)}, u32[]{:S(2)}) collective-permute-start(bf16[32,1024]{1,0:T(8,128)(2,1)S(1)} %bitcast.58), channel_id=1, source_target_pairs={{1,0},{2,1},{3,2},{4,3},{5,4},{6,5},{7,6},{8,7},{9,8},{10,9},{11,1... | collective-permute-start | bytes 196616 | tf_op jit(solution)/shard_map/ppermute | solution.py:15
Sparse Core Ops, SparseCore 0:
  10.3 387.5 all-gather.2
where the time goes:
time: 416 us
  waiting for transfers between devices  361 us (87%)
  starting transfers between devices  15.2 us (4%)
  between operations  13.6 us (3%)
  local copies, waits for them, and re-layouts  13.1 us (3%)
  matrix products  10.5 us (3%)
    all_gather x1, waiting for transfers between devices, body(): lax.all_gather(coarse_flat, ('wide', 'narrow'), axis=0, tiled=True)  361 us
    ppermute x2, starting transfers between devices, with_halo(): lax.ppermute(lax.slice_in_dim(block, block.shape[dim] - width, None, axis...  11.3 us
  transfers between devices with their start and end apart: 5, of which 1 were waited for; matrix products, arithmetic and copies ran while one was open for 3% of the time, Pallas kernels for 0%

commit v1 on v0

--- a/solution.py
+++ b/solution.py
@@ -1,7 +1,10 @@
 import jax
 import jax.numpy as jnp
 from jax import lax
-from jax.sharding import PartitionSpec as P
+from jax.sharding import Mesh, PartitionSpec as P
+
+ALL = ("z", "x", "y_lo", "y_hi", "core")
+STAGES = (("z",), ("x", "y_lo", "y_hi"), ("core",))
 
 
 def with_halo(block, sides, width):
@@ -45,12 +48,18 @@
         preferred_element_type=jnp.float32,
     ).astype(jnp.bfloat16)
     coarse_flat = coarse.reshape(box_count, rhs_count * rank_width)
-    everything = lax.all_gather(coarse_flat, ("wide", "narrow"), axis=0, tiled=True)
-    offset_base = lax.axis_index(("wide", "narrow")) * leaf_count - leaf_count
+    everything = coarse_flat
+    for axes in STAGES:
+        n = lax.axis_size(axes)
+        spread = jnp.broadcast_to(everything[None], (n,) + everything.shape)
+        everything = lax.all_to_all(spread, axes, 0, 0, tiled=False).reshape(
+            (n * everything.shape[0],) + everything.shape[1:]
+        )
+    offset_base = lax.axis_index(ALL) * leaf_count - leaf_count
     density_flat = density.reshape(leaf_count, rhs_count * leaf_width)
     skeleton_flat = skeleton.reshape(leaf_count, rhs_count * rank_width)
-    density_padded = with_halo(density_flat, ((("wide", "narrow"), 0),), leaf_count)
-    skeleton_padded = with_halo(skeleton_flat, ((("wide", "narrow"), 0),), leaf_count)
+    density_padded = with_halo(density_flat, ((ALL, 0),), leaf_count)
+    skeleton_padded = with_halo(skeleton_flat, ((ALL, 0),), leaf_count)
     near_rows = jnp.take(density_padded, near_list - offset_base, axis=0).reshape(
         leaf_count, near_list.shape[1], rhs_count, leaf_width
     )
@@ -66,7 +75,18 @@
         far_skels,
         preferred_element_type=jnp.float32,
     )
-    coarse_skels = jnp.take(everything, far_coarse, axis=0).reshape(
+    sizes = [lax.axis_size(a) for a in ALL]
+    owner, slot = far_coarse // box_count, far_coarse % box_count
+    coords = []
+    for size in reversed(sizes):
+        coords.append(owner % size)
+        owner = owner // size
+    coords = dict(zip(reversed(ALL), coords))
+    position = 0
+    for axes in reversed(STAGES):
+        for a in axes:
+            position = position * lax.axis_size(a) + coords[a]
+    coarse_skels = jnp.take(everything, position * box_count + slot, axis=0).reshape(
         box_count, coarse_count, rhs_count, rank_width
     )
     coarse_field = jnp.einsum(
@@ -90,20 +110,22 @@
 
 
 def solution(mesh):
+    assert tuple(mesh.shape.values()) == (64, 4)
+    grid = Mesh(mesh.devices.reshape(8, 4, 2, 2, 2), ALL)
     return jax.shard_map(
         body,
-        mesh=mesh,
+        mesh=grid,
         in_specs=(
-            P(("wide", "narrow"), None, None),
-            P(("wide", "narrow"), None, None),
-            P(("wide", "narrow"), None),
-            P(("wide", "narrow"), None, None, None),
-            P(("wide", "narrow"), None),
-            P(("wide", "narrow"), None, None),
-            P(("wide", "narrow"), None, None),
-            P(("wide", "narrow"), None),
-            P(("wide", "narrow"), None, None),
+            P(ALL, None, None),
+            P(ALL, None, None),
+            P(ALL, None),
+            P(ALL, None, None, None),
+            P(ALL, None),
+            P(ALL, None, None),
+            P(ALL, None, None),
+            P(ALL, None),
+            P(ALL, None, None),
         ),
-        out_specs=P(("wide", "narrow"), None, None),
+        out_specs=P(ALL, None, None),
         check_vma=False,
     )

time: 416 us -> 74.4 us (0.18)
  waiting for transfers between devices: 361 us -> 6.07 us
  starting transfers between devices: 15.2 us -> 30.6 us
  between operations: 13.6 us -> 0.16 us
  blocking collectives: 0 us -> 11.4 us
    all_gather x1 -> x0, waiting for transfers between devices: 361 us -> none  [body(): lax.all_gather(coarse_flat, ('wide', 'narrow'), axis=0, tiled=True)]
    all_to_all x0 -> x2, starting transfers between devices: none -> 15.4 us  [body(): lax.all_to_all(spread, axes, 0, 0, tiled=False)]
    all_to_all x0 -> x1, blocking collectives: none -> 11.4 us  [body(): lax.all_to_all(spread, axes, 0, 0, tiled=False)]
    all_to_all x0 -> x2, waiting for transfers between devices: none -> 6.06 us  [body(): lax.all_to_all(spread, axes, 0, 0, tiled=False)]
  transfers between devices with their start and end apart: 5 -> 6, of which waited for: 1 -> 2; matrix products, arithmetic and copies ran while one was open for 3% -> 18% of each run, Pallas kernels for 0% -> 0%
where the time goes in v1:
time: 74.4 us; the launch traced here: 73.7 us
  starting transfers between devices  30.6 us (41%)
  local copies, waits for them, and re-layouts  13.8 us (19%)
  blocking collectives  11.4 us (15%)
  matrix products  10.2 us (14%)
  waiting for transfers between devices  6.07 us (8%)
  other arithmetic  1.49 us (2%)
    all_to_all x2, starting transfers between devices, body(): lax.all_to_all(spread, axes, 0, 0, tiled=False)  15.4 us
    all_to_all x1, blocking collectives, body(): lax.all_to_all(spread, axes, 0, 0, tiled=False)  11.4 us
    ppermute x2, starting transfers between devices, with_halo(): lax.ppermute(lax.slice_in_dim(block, block.shape[dim] - width, None, axis...  11.3 us
    all_to_all x2, waiting for transfers between devices, body(): lax.all_to_all(spread, axes, 0, 0, tiled=False)  6.06 us
    dot_general x1, matrix products, body(): jnp.einsum('ljpq,ljrq->lrp', near_blocks, near_rows, preferred_element_ty...  5.2 us
    reshape x1, local copies, waits for them, and re-layouts, body(): leaf_coupling.reshape(leaf_count, rank_width, far_count, rank_width)  4.11 us
    ppermute x2, starting transfers between devices, with_halo(): lax.ppermute(lax.slice_in_dim(block, 0, width, axis=dim), axis, backward)  3.84 us
    dot_general x1, matrix products, body(): jnp.einsum('lrk,lkp->lrp', local_field, basis, preferred_element_type=jnp...  3.09 us
  transfers between devices with their start and end apart: 6, of which 2 were waited for; matrix products, arithmetic and copies ran while one was open for 18% of the time, Pallas kernels for 0%

profile of v1, /device:TPU:1, one launch (start us, length us, event | category | flops | bytes accessed | tf_op | source)
XLA Modules:
  0.0 73.7 jit_solution(3032780546301045155)
XLA Ops:
  0.0 1.0 %copy-done = bf16[32,64,128]{2,1,0:T(8,128)(2,1)S(1)} copy-done((bf16[32,64,128]{2,1,0:T(8,128)(2,1)S(1)}, bf16[32,64,128]{2,1,0:T(8,128)(2,1)}, u32[]{:S(2)}) %copy-start) | copy-done | bytes 524312
  1.0 1.2 %convolution_convert_fusion = bf16[32,8,64]{2,1,0:T(8,128)(2,1)S(1)} fusion(bf16[32,8,128]{2,1,0:T(8,128)(2,1)} %param.9, bf16[32,64,128]{2,1,0:T(8,128)(2,1)S(1)} %copy-done), kind=kOutput, calls=%fused_computation.9 | convolution fusion | flops 4210688 | bytes 622592 | tf_op jit(solution)/shard_map/lrp,lkp->lrk/dot_general | solution.py:40
  2.4 6.2 %collective-permute-start = (bf16[32,512]{1,0:T(8,128)(2,1)S(1)}, bf16[32,512]{1,0:T(8,128)(2,1)S(1)}, u32[]{:S(2)}, u32[]{:S(2)}) collective-permute-start(bf16[32,512]{1,0:T(8,128)(2,1)S(1)} %reshape.49), channel_id=1, source_target_pairs={{0,1},{1,2},{2,3},{3,4},{4,5},{5,6},{6,7},{7,8},{8,9},{9,10},{10,1... | collective-permute-start | bytes 98312 | tf_op jit(solution)/shard_map/ppermute | solution.py:15
  8.6 1.9 %collective-permute-start.1 = (bf16[32,512]{1,0:T(8,128)(2,1)S(1)}, bf16[32,512]{1,0:T(8,128)(2,1)S(1)}, u32[]{:S(2)}, u32[]{:S(2)}) collective-permute-start(bf16[32,512]{1,0:T(8,128)(2,1)S(1)} %reshape.49), channel_id=1, source_target_pairs={{1,0},{2,1},{3,2},{4,3},{5,4},{6,5},{7,6},{8,7},{9,8},{10,9},{11,1... | collective-permute-start | bytes 98312 | tf_op jit(solution)/shard_map/ppermute | solution.py:18
  10.5 0.9 %copy.36 = bf16[4,8,8,128]{3,1,2,0:T(8,128)(2,1)S(1)} copy(bf16[4,8,8,128]{3,2,1,0:T(8,128)(2,1)} %bitcast.66) | data formatting | bytes 131072
  11.4 5.1 %collective-permute-start.2 = (bf16[32,1024]{1,0:T(8,128)(2,1)S(1)}, bf16[32,1024]{1,0:T(8,128)(2,1)S(1)}, u32[]{:S(2)}, u32[]{:S(2)}) collective-permute-start(bf16[32,1024]{1,0:T(8,128)(2,1)S(1)} %bitcast.67), channel_id=1, source_target_pairs={{0,1},{1,2},{2,3},{3,4},{4,5},{5,6},{6,7},{7,8},{8,9},{9,10},{10,1... | collective-permute-start | bytes 196616 | tf_op jit(solution)/shard_map/ppermute | solution.py:15
  16.5 1.9 %collective-permute-start.3 = (bf16[32,1024]{1,0:T(8,128)(2,1)S(1)}, bf16[32,1024]{1,0:T(8,128)(2,1)S(1)}, u32[]{:S(2)}, u32[]{:S(2)}) collective-permute-start(bf16[32,1024]{1,0:T(8,128)(2,1)S(1)} %bitcast.68), channel_id=1, source_target_pairs={{1,0},{2,1},{3,2},{4,3},{5,4},{6,5},{7,6},{8,7},{9,8},{10,9},{11,1... | collective-permute-start | bytes 196616 | tf_op jit(solution)/shard_map/ppermute | solution.py:18
  18.5 1.3 %reshape.52 = bf16[4,64,8,64]{3,2,1,0:T(8,128)(2,1)S(1)} reshape(bf16[4,64,512]{2,1,0:T(8,128)(2,1)} %param.15) | data formatting | bytes 524288 | tf_op jit(solution)/shard_map/reshape | solution.py:46
  20.1 0.6 broadcast_in_dim.62
  20.7 9.3 %all-to-all-start = ((bf16[8,4,512]{2,1,0:T(4,128)(2,1)}), bf16[8,4,512]{2,1,0:T(4,128)(2,1)S(1)}, u32[]{:S(2)}, u32[]{:S(2)}) async-start(bf16[8,4,512]{2,1,0:T(4,128)(2,1)} %broadcast_in_dim.62), calls=%async_computation | async-start | bytes 65536 | tf_op jit(solution)/shard_map/all_to_all | solution.py:55
  30.0 0.7 compare_and_fusion
  30.7 0.7 compare_and_fusion.2
  31.7 5.2 %all-to-all-done = bf16[8,4,512]{2,1,0:T(4,128)(2,1)S(1)} async-done(((bf16[8,4,512]{2,1,0:T(4,128)(2,1)}), bf16[8,4,512]{2,1,0:T(4,128)(2,1)S(1)}, u32[]{:S(2)}, u32[]{:S(2)}) %all-to-all-start) | async-done | bytes 32800 | tf_op jit(solution)/shard_map/all_to_all | solution.py:55
  36.9 0.9 %broadcast_in_dim.64 = bf16[16,32,512]{2,1,0:T(8,128)(2,1)} broadcast(bf16[32,512]{1,0:T(8,128)(2,1)S(1)} %broadcast_in_dim.63), dimensions={1,2} | broadcast | bytes 557056 | tf_op jit(solution)/shard_map/broadcast_in_dim | solution.py:54
  37.8 6.1 %all-to-all-start.1 = ((bf16[16,32,512]{2,1,0:T(8,128)(2,1)}), bf16[16,32,512]{2,1,0:T(8,128)(2,1)S(1)}, u32[]{:S(2)}, u32[]{:S(2)}) async-start(bf16[16,32,512]{2,1,0:T(8,128)(2,1)} %broadcast_in_dim.64), calls=%async_computation.1 | async-start | bytes 1048576 | tf_op jit(solution)/shard_map/all_to_all | solution.py:55
  44.5 4.1 %copy.27 = bf16[32,64,384]{1,2,0:T(8,128)(2,1)} copy(bf16[32,64,384]{2,1,0:T(8,128)(2,1)} %param.14) | data formatting | bytes 3145728 | tf_op jit(solution)/shard_map/reshape | solution.py:74
  48.8 1.0 %gather_fusion = bf16[192,512]{1,0:T(8,128)(2,1)S(1)} fusion(bf16[96,512]{1,0:T(8,128)(2,1)S(1)} %pad_maximum_fusion.1, s32[1024]{0:T(1024)S(1)} %pad_clamp_fusion.2), kind=kCustom, calls=%fused_computation | custom fusion | bytes 393984 | tf_op jit(solution)/shard_map/jit(_take)/gather | solution.py:69
  50.1 1.0 %gather_fusion.2 = bf16[192,1024]{1,0:T(8,128)(2,1)S(1)} fusion(bf16[96,1024]{1,0:T(8,128)(2,1)S(1)} %pad_maximum_fusion, s32[1024]{0:T(1024)S(1)} %pad_clamp_fusion), kind=kCustom, calls=%fused_computation.2 | custom fusion | bytes 787200 | tf_op jit(solution)/shard_map/jit(_take)/gather | solution.py:63
  51.1 0.8 %copy.30 = bf16[24,8,8,128]{3,2,1,0:T(8,128)(2,1)} copy(bf16[24,8,8,128]{3,1,2,0:T(8,128)(2,1)S(1)} %bitcast.59) | data formatting | bytes 786432
  51.9 0.8 %all-to-all-done.1 = bf16[16,32,512]{2,1,0:T(8,128)(2,1)S(1)} async-done(((bf16[16,32,512]{2,1,0:T(8,128)(2,1)}), bf16[16,32,512]{2,1,0:T(8,128)(2,1)S(1)}, u32[]{:S(2)}, u32[]{:S(2)}) %all-to-all-start.1) | async-done | bytes 524320 | tf_op jit(solution)/shard_map/all_to_all | solution.py:55
  52.8 11.4 %all_to_all.15 = bf16[2,512,512]{2,1,0:T(8,128)(2,1)S(1)} all-to-all(bf16[2,512,512]{2,1,0:T(8,128)(2,1)S(1)} %broadcast_in_dim.66), channel_id=1, replica_groups=mesh['z'=8,'x'=4,'y_lo'=2,'y_hi'=2,'core'=2] {'core'}, dimensions={0} | all-to-all | bytes 2097152 | tf_op jit(solution)/shard_map/all_to_all | solution.py:55
  64.2 0.6 gather_fusion.1
  65.4 3.1 %fusion.4 = f32[32,8,128]{2,1,0:T(8,128)S(1)} fusion(bf16[32,64,128]{2,1,0:T(8,128)(2,1)S(1)} %copy-done, f32[32,8,64]{2,1,0:T(8,128)S(1)} %bitcast.65, bf16[32,64,6,64]{1,3,2,0:T(8,128)(2,1)} %bitcast.58, bf16[32,6,8,64]{3,2,1,0:T(8,128)(2,1)S(1)} %gather.19, pred[32,6]{1,0:T(8,128)(4,1)S(1)} %copy.14), kind=kOutput, calls=%fused_computation.10 | convolution fusion | flops 16908288 | bytes 2490560 | tf_op jit(solution)/shard_map/lrk,lkp->lrp/dot_general | solution.py:106
  68.5 5.2 %fusion.3 = bf16[32,8,128]{2,1,0:T(8,128)(2,1)} fusion(f32[32,8,128]{2,1,0:T(8,128)S(1)} %fusion.4, bf16[32,6,128,128]{3,2,1,0:T(8,128)(2,1)} %param.12, bf16[32,6,8,128]{3,2,1,0:T(8,128)(2,1)S(1)} %bitcast.63, pred[32,6]{1,0:T(8,128)(4,1)S(1)} %copy.18), kind=kOutput, calls=%fused_computation.8 | convolution fusion | flops 50593792 | bytes 6881472 | tf_op jit(solution)/shard_map/ljpq,ljrq->lrp/dot_general | solution.py:66
  (30 shorter events, 2.3 us)
Async XLA Ops:
  0.0 1.0 %copy-start = (bf16[32,64,128]{2,1,0:T(8,128)(2,1)S(1)}, bf16[32,64,128]{2,1,0:T(8,128)(2,1)}, u32[]{:S(2)}) copy-start(bf16[32,64,128]{2,1,0:T(8,128)(2,1)} %param.10) | copy-start | bytes 1572868
  0.0 44.3 %copy-start.2 = (bf16[4,64,512]{2,1,0:T(8,128)(2,1)S(1)}, bf16[4,64,512]{2,1,0:T(8,128)(2,1)}, u32[]{:S(2)}) copy-start(bf16[4,64,512]{2,1,0:T(8,128)(2,1)} %param.17) | copy-start | bytes 786436
  2.4 46.4 %collective-permute-start = (bf16[32,512]{1,0:T(8,128)(2,1)S(1)}, bf16[32,512]{1,0:T(8,128)(2,1)S(1)}, u32[]{:S(2)}, u32[]{:S(2)}) collective-permute-start(bf16[32,512]{1,0:T(8,128)(2,1)S(1)} %reshape.49), channel_id=1, source_target_pairs={{0,1},{1,2},{2,3},{3,4},{4,5},{5,6},{6,7},{7,8},{8,9},{9,10},{10,1... | collective-permute-start | bytes 98312 | tf_op jit(solution)/shard_map/ppermute | solution.py:15
  8.6 40.2 %collective-permute-start.1 = (bf16[32,512]{1,0:T(8,128)(2,1)S(1)}, bf16[32,512]{1,0:T(8,128)(2,1)S(1)}, u32[]{:S(2)}, u32[]{:S(2)}) collective-permute-start(bf16[32,512]{1,0:T(8,128)(2,1)S(1)} %reshape.49), channel_id=1, source_target_pairs={{1,0},{2,1},{3,2},{4,3},{5,4},{6,5},{7,6},{8,7},{9,8},{10,9},{11,1... | collective-permute-start | bytes 98312 | tf_op jit(solution)/shard_map/ppermute | solution.py:18
  11.4 38.6 %collective-permute-start.2 = (bf16[32,1024]{1,0:T(8,128)(2,1)S(1)}, bf16[32,1024]{1,0:T(8,128)(2,1)S(1)}, u32[]{:S(2)}, u32[]{:S(2)}) collective-permute-start(bf16[32,1024]{1,0:T(8,128)(2,1)S(1)} %bitcast.67), channel_id=1, source_target_pairs={{0,1},{1,2},{2,3},{3,4},{4,5},{5,6},{6,7},{7,8},{8,9},{9,10},{10,1... | collective-permute-start | bytes 196616 | tf_op jit(solution)/shard_map/ppermute | solution.py:15
  16.5 33.5 %collective-permute-start.3 = (bf16[32,1024]{1,0:T(8,128)(2,1)S(1)}, bf16[32,1024]{1,0:T(8,128)(2,1)S(1)}, u32[]{:S(2)}, u32[]{:S(2)}) collective-permute-start(bf16[32,1024]{1,0:T(8,128)(2,1)S(1)} %bitcast.68), channel_id=1, source_target_pairs={{1,0},{2,1},{3,2},{4,3},{5,4},{6,5},{7,6},{8,7},{9,8},{10,9},{11,1... | collective-permute-start | bytes 196616 | tf_op jit(solution)/shard_map/ppermute | solution.py:18
  20.7 16.2 %all-to-all-start = ((bf16[8,4,512]{2,1,0:T(4,128)(2,1)}), bf16[8,4,512]{2,1,0:T(4,128)(2,1)S(1)}, u32[]{:S(2)}, u32[]{:S(2)}) async-start(bf16[8,4,512]{2,1,0:T(4,128)(2,1)} %broadcast_in_dim.62), calls=%async_computation | async-start | bytes 65536 | tf_op jit(solution)/shard_map/all_to_all | solution.py:55
  37.8 15.0 %all-to-all-start.1 = ((bf16[16,32,512]{2,1,0:T(8,128)(2,1)}), bf16[16,32,512]{2,1,0:T(8,128)(2,1)S(1)}, u32[]{:S(2)}, u32[]{:S(2)}) async-start(bf16[16,32,512]{2,1,0:T(8,128)(2,1)} %broadcast_in_dim.64), calls=%async_computation.1 | async-start | bytes 1048576 | tf_op jit(solution)/shard_map/all_to_all | solution.py:55
  64.2 4.3 %copy-start.1 = (bf16[24,8,8,128]{3,2,1,0:T(8,128)(2,1)S(1)}, bf16[24,8,8,128]{3,2,1,0:T(8,128)(2,1)}, u32[]{:S(2)}) copy-start(bf16[24,8,8,128]{3,2,1,0:T(8,128)(2,1)} %copy.30) | copy-start | bytes 1179652

commit v2 on v1

--- a/solution.py
+++ b/solution.py
@@ -4,7 +4,8 @@
 from jax.sharding import Mesh, PartitionSpec as P
 
 ALL = ("z", "x", "y_lo", "y_hi", "core")
-STAGES = (("z",), ("x", "y_lo", "y_hi"), ("core",))
+STAGES = (("z",), ("x", "y_lo", "y_hi"))
+PAIR = "core"
 
 
 def with_halo(block, sides, width):
@@ -55,11 +56,16 @@
         everything = lax.all_to_all(spread, axes, 0, 0, tiled=False).reshape(
             (n * everything.shape[0],) + everything.shape[1:]
         )
+    partner = lax.ppermute(everything, PAIR, [(0, 1), (1, 0)])
+    everything = jnp.concatenate([everything, partner], axis=0)
     offset_base = lax.axis_index(ALL) * leaf_count - leaf_count
     density_flat = density.reshape(leaf_count, rhs_count * leaf_width)
     skeleton_flat = skeleton.reshape(leaf_count, rhs_count * rank_width)
-    density_padded = with_halo(density_flat, ((ALL, 0),), leaf_count)
-    skeleton_padded = with_halo(skeleton_flat, ((ALL, 0),), leaf_count)
+    both_padded = with_halo(
+        jnp.concatenate([density_flat, skeleton_flat], axis=1), ((ALL, 0),), leaf_count
+    )
+    density_padded = both_padded[:, : density_flat.shape[1]]
+    skeleton_padded = both_padded[:, density_flat.shape[1] :]
     near_rows = jnp.take(density_padded, near_list - offset_base, axis=0).reshape(
         leaf_count, near_list.shape[1], rhs_count, leaf_width
     )
@@ -82,7 +88,7 @@
         coords.append(owner % size)
         owner = owner // size
     coords = dict(zip(reversed(ALL), coords))
-    position = 0
+    position = (coords[PAIR] != lax.axis_index(PAIR)).astype(jnp.int32)
     for axes in reversed(STAGES):
         for a in axes:
             position = position * lax.axis_size(a) + coords[a]

time: 74.4 us -> 59 us (0.79)
  blocking collectives: 11.4 us -> 0 us
  starting transfers between devices: 30.6 us -> 28.1 us
  local copies, waits for them, and re-layouts: 13.8 us -> 12.8 us
    all_to_all x1 -> x0, blocking collectives: 11.4 us -> none  [body(): lax.all_to_all(spread, axes, 0, 0, tiled=False)]
    ppermute x2 -> x1, starting transfers between devices: 11.3 us -> 7.32 us  [with_halo(): lax.ppermute(lax.slice_in_dim(block, block.shape[dim] - width, None, axis...]
    ppermute x0 -> x1, starting transfers between devices: none -> 3.07 us  [body(): partner = lax.ppermute(everything, PAIR, [(0, 1), (1, 0)])]
    ppermute x2 -> x1, starting transfers between devices: 3.84 us -> 1.92 us  [with_halo(): lax.ppermute(lax.slice_in_dim(block, 0, width, axis=dim), axis, backward)]
    concatenate x0 -> x1, other arithmetic: none -> 1.11 us  [body(): everything = jnp.concatenate([everything, partner], axis=0)]
    unnamed x8 -> x14, local copies, waits for them, and re-layouts: 2.72 us -> 1.68 us
    broadcast_in_dim x5 -> x4, local copies, waits for them, and re-layouts: 1.68 us -> 1.6 us  [body(): spread = jnp.broadcast_to(everything[None], (n,) + everything.shape)]
  transfers between devices with their start and end apart: 6 -> 5, of which waited for: 2 -> 1; matrix products, arithmetic and copies ran while one was open for 18% -> 16% of each run, Pallas kernels for 0% -> 0%
where the time goes in v2:
time: 59 us; the launch traced here: 58.4 us
  starting transfers between devices  28.1 us (48%)
  local copies, waits for them, and re-layouts  12.8 us (22%)
  matrix products  10.2 us (17%)
  waiting for transfers between devices  5.92 us (10%)
  other arithmetic  1.22 us (2%)
    all_to_all x2, starting transfers between devices, body(): lax.all_to_all(spread, axes, 0, 0, tiled=False)  15.8 us
    ppermute x1, starting transfers between devices, with_halo(): lax.ppermute(lax.slice_in_dim(block, block.shape[dim] - width, None, axis...  7.32 us
    all_to_all x2, waiting for transfers between devices, body(): lax.all_to_all(spread, axes, 0, 0, tiled=False)  5.91 us
    dot_general x1, matrix products, body(): jnp.einsum('ljpq,ljrq->lrp', near_blocks, near_rows, preferred_element_ty...  5.2 us
    reshape x1, local copies, waits for them, and re-layouts, body(): leaf_coupling.reshape(leaf_count, rank_width, far_count, rank_width)  4.15 us
    dot_general x1, matrix products, body(): jnp.einsum('lrk,lkp->lrp', local_field, basis, preferred_element_type=jnp...  3.09 us
    ppermute x1, starting transfers between devices, body(): partner = lax.ppermute(everything, PAIR, [(0, 1), (1, 0)])  3.07 us
    ppermute x1, starting transfers between devices, with_halo(): lax.ppermute(lax.slice_in_dim(block, 0, width, axis=dim), axis, backward)  1.92 us
  transfers between devices with their start and end apart: 5, of which 1 were waited for; matrix products, arithmetic and copies ran while one was open for 16% of the time, Pallas kernels for 0%

profile of v2, /device:TPU:1, one launch (start us, length us, event | category | flops | bytes accessed | tf_op | source)
XLA Modules:
  0.0 58.4 jit_solution(9003855498303287678)
XLA Ops:
  0.0 1.3 %reshape.52 = bf16[4,64,8,64]{3,2,1,0:T(8,128)(2,1)S(1)} reshape(bf16[4,64,512]{2,1,0:T(8,128)(2,1)} %param.15) | data formatting | bytes 524288 | tf_op jit(solution)/shard_map/reshape | solution.py:47
  1.4 1.2 %convolution_convert_fusion = bf16[32,8,64]{2,1,0:T(8,128)(2,1)S(1)} fusion(bf16[32,8,128]{2,1,0:T(8,128)(2,1)} %param.9, bf16[32,64,128]{2,1,0:T(8,128)(2,1)S(1)} %copy-done), kind=kOutput, calls=%fused_computation.9 | convolution fusion | flops 4210688 | bytes 622592 | tf_op jit(solution)/shard_map/lrp,lkp->lrk/dot_general | solution.py:41
  2.6 0.3 fusion.5
  2.9 0.6 %broadcast_in_dim.55 = bf16[8,4,512]{2,1,0:T(4,128)(2,1)} broadcast(bf16[4,512]{1,0:T(4,128)(2,1)S(1)} %broadcast_in_dim.54), dimensions={1,2} | broadcast | bytes 36864 | tf_op jit(solution)/shard_map/broadcast_in_dim | solution.py:55
  3.6 9.0 %all-to-all-start = ((bf16[8,4,512]{2,1,0:T(4,128)(2,1)}), bf16[8,4,512]{2,1,0:T(4,128)(2,1)S(1)}, u32[]{:S(2)}, u32[]{:S(2)}) async-start(bf16[8,4,512]{2,1,0:T(4,128)(2,1)} %broadcast_in_dim.55), calls=%async_computation | async-start | bytes 65536 | tf_op jit(solution)/shard_map/all_to_all | solution.py:56
  12.6 0.8 %bitcast_dynamic-update-slice_fusion = bf16[32,1536]{1,0:T(8,128)(2,1)S(1)} fusion(bf16[4,8,8,128]{3,2,1,0:T(8,128)(2,1)} %bitcast.64), kind=kLoop, calls=%fused_computation.29 | loop fusion | bytes 131072
  13.4 0.1 reshape.49
  13.5 5.9 %all-to-all-done = bf16[8,4,512]{2,1,0:T(4,128)(2,1)S(1)} async-done(((bf16[8,4,512]{2,1,0:T(4,128)(2,1)}), bf16[8,4,512]{2,1,0:T(4,128)(2,1)S(1)}, u32[]{:S(2)}, u32[]{:S(2)}) %all-to-all-start) | async-done | bytes 32800 | tf_op jit(solution)/shard_map/all_to_all | solution.py:56
  19.5 0.8 %broadcast_in_dim.57 = bf16[16,32,512]{2,1,0:T(8,128)(2,1)} broadcast(bf16[32,512]{1,0:T(8,128)(2,1)S(1)} %broadcast_in_dim.56), dimensions={1,2} | broadcast | bytes 557056 | tf_op jit(solution)/shard_map/broadcast_in_dim | solution.py:55
  20.3 6.8 %all-to-all-start.1 = ((bf16[16,32,512]{2,1,0:T(8,128)(2,1)}), bf16[16,32,512]{2,1,0:T(8,128)(2,1)S(1)}, u32[]{:S(2)}, u32[]{:S(2)}) async-start(bf16[16,32,512]{2,1,0:T(8,128)(2,1)} %broadcast_in_dim.57), calls=%async_computation.1 | async-start | bytes 1048576 | tf_op jit(solution)/shard_map/all_to_all | solution.py:56
  27.1 7.3 %collective-permute-start = (bf16[32,1536]{1,0:T(8,128)(2,1)S(1)}, bf16[32,1536]{1,0:T(8,128)(2,1)S(1)}, u32[]{:S(2)}, u32[]{:S(2)}) collective-permute-start(bf16[32,1536]{1,0:T(8,128)(2,1)S(1)} %constant_dynamic-update-slice_fusion), channel_id=1, source_target_pairs={{0,1},{1,2},{2,3},{3,4},{4,5},{5,6},{6,7},{7,8},{8,9},{9,10},{10,1... | collective-permute-start | bytes 294920 | tf_op jit(solution)/shard_map/ppermute | solution.py:16
  34.4 1.9 %collective-permute-start.1 = (bf16[32,1536]{1,0:T(8,128)(2,1)S(1)}, bf16[32,1536]{1,0:T(8,128)(2,1)S(1)}, u32[]{:S(2)}, u32[]{:S(2)}) collective-permute-start(bf16[32,1536]{1,0:T(8,128)(2,1)S(1)} %constant_dynamic-update-slice_fusion), channel_id=1, source_target_pairs={{1,0},{2,1},{3,2},{4,3},{5,4},{6,5},{7,6},{8,7},{9,8},{10,9},{11,1... | collective-permute-start | bytes 294920 | tf_op jit(solution)/shard_map/ppermute | solution.py:19
  36.4 3.1 %collective-permute-start.2 = (bf16[512,512]{1,0:T(8,128)(2,1)S(1)}, bf16[512,512]{1,0:T(8,128)(2,1)}, u32[]{:S(2)}, u32[]{:S(2)}) collective-permute-start(bf16[512,512]{1,0:T(8,128)(2,1)S(1)} %bitcast.59), channel_id=1, source_target_pairs={{0,1},{1,0},{2,3},{3,2},{4,5},{5,4},{6,7},{7,6},{8,9},{9,8},{10,11... | collective-permute-start | bytes 1572872 | tf_op jit(solution)/shard_map/ppermute | solution.py:59
  40.1 0.3 copy.28
  40.4 4.2 %copy.27 = bf16[32,64,384]{1,2,0:T(8,128)(2,1)} copy(bf16[32,64,384]{2,1,0:T(8,128)(2,1)} %param.14) | data formatting | bytes 3145728 | tf_op jit(solution)/shard_map/reshape | solution.py:80
  44.7 1.0 %gather_fusion = bf16[192,512]{1,0:T(8,128)(2,1)S(1)} fusion(bf16[96,512]{1,0:T(8,128)(2,1)S(1)} %pad_maximum_fusion.3, s32[1024]{0:T(1024)S(1)} %get-tuple-element.12), kind=kCustom, calls=%fused_computation | custom fusion | bytes 393984 | tf_op jit(solution)/shard_map/jit(_take)/gather | solution.py:75
  45.7 0.2 gather.19
  46.0 1.0 %gather_fusion.2 = bf16[192,1024]{1,0:T(8,128)(2,1)S(1)} fusion(bf16[96,1024]{1,0:T(8,128)(2,1)S(1)} %pad_maximum_fusion.1, s32[1024]{0:T(1024)S(1)} %get-tuple-element.11), kind=kCustom, calls=%fused_computation.2 | custom fusion | bytes 787200 | tf_op jit(solution)/shard_map/jit(_take)/gather | solution.py:69
  47.0 0.8 %copy.30 = bf16[24,8,8,128]{3,2,1,0:T(8,128)(2,1)} copy(bf16[24,8,8,128]{3,1,2,0:T(8,128)(2,1)S(1)} %bitcast.57) | data formatting | bytes 786432
  47.8 1.1 %pad_maximum_fusion = bf16[1024,512]{1,0:T(8,128)(2,1)S(1)} fusion(bf16[512,512]{1,0:T(8,128)(2,1)} %collective-permute-done.2, bf16[512,512]{1,0:T(8,128)(2,1)S(1)} %bitcast.60), kind=kLoop, calls=%fused_computation.16 | loop fusion | flops 2097152 | bytes 2097152 | tf_op jit(solution)/shard_map/concatenate | solution.py:60
  49.0 0.6 %gather_fusion.1 = bf16[32,512]{1,0:T(8,128)(2,1)S(1)} fusion(bf16[1024,512]{1,0:T(8,128)(2,1)S(1)} %pad_maximum_fusion, s32[1024]{0:T(1024)S(1)} %pad_clamp_fusion.1), kind=kCustom, calls=%fused_computation.1 | custom fusion | bytes 65664 | tf_op jit(solution)/shard_map/jit(_take)/gather | solution.py:95
  49.7 0.5 fusion.8
  50.2 3.1 %fusion.4 = f32[32,8,128]{2,1,0:T(8,128)S(1)} fusion(bf16[32,64,128]{2,1,0:T(8,128)(2,1)S(1)} %copy-done, f32[32,8,64]{2,1,0:T(8,128)S(1)} %bitcast.63, bf16[32,64,6,64]{1,3,2,0:T(8,128)(2,1)} %bitcast.56, bf16[32,6,8,64]{3,2,1,0:T(8,128)(2,1)S(1)} %gather.19, pred[32,6]{1,0:T(8,128)(4,1)S(1)} %copy.14), kind=kOutput, calls=%fused_computation.10 | convolution fusion | flops 16908288 | bytes 2490560 | tf_op jit(solution)/shard_map/lrk,lkp->lrp/dot_general | solution.py:112
  53.2 5.2 %fusion.3 = bf16[32,8,128]{2,1,0:T(8,128)(2,1)} fusion(f32[32,8,128]{2,1,0:T(8,128)S(1)} %fusion.4, bf16[32,6,128,128]{3,2,1,0:T(8,128)(2,1)} %param.12, bf16[32,6,8,128]{3,2,1,0:T(8,128)(2,1)S(1)} %bitcast.61, pred[32,6]{1,0:T(8,128)(4,1)S(1)} %copy.18), kind=kOutput, calls=%fused_computation.8 | convolution fusion | flops 50593792 | bytes 6881472 | tf_op jit(solution)/shard_map/ljpq,ljrq->lrp/dot_general | solution.py:72
  (34 shorter events, 1.0 us)
Async XLA Ops:
  0.0 1.4 %copy-start = (bf16[32,64,128]{2,1,0:T(8,128)(2,1)S(1)}, bf16[32,64,128]{2,1,0:T(8,128)(2,1)}, u32[]{:S(2)}) copy-start(bf16[32,64,128]{2,1,0:T(8,128)(2,1)} %param.10) | copy-start | bytes 1572868
  0.0 36.4 %copy-start.3 = (s32[32,6]{0,1:T(8,128)S(1)}, s32[32,6]{0,1:T(8,128)}, u32[]{:S(2)}) copy-start(s32[32,6]{0,1:T(8,128)} %param.13) | copy-start | bytes 2308
  0.0 36.4 %copy-start.4 = (s32[32,6]{0,1:T(8,128)S(1)}, s32[32,6]{0,1:T(8,128)}, u32[]{:S(2)}) copy-start(s32[32,6]{0,1:T(8,128)} %param.11) | copy-start | bytes 2308
  0.0 39.5 %copy-start.5 = (s32[4,8]{1,0:T(4,128)S(1)}, s32[4,8]{1,0:T(4,128)}, u32[]{:S(2)}) copy-start(s32[4,8]{1,0:T(4,128)} %param.16) | copy-start | bytes 388
  0.0 40.1 %copy-start.2 = (bf16[4,64,512]{2,1,0:T(8,128)(2,1)S(1)}, bf16[4,64,512]{2,1,0:T(8,128)(2,1)}, u32[]{:S(2)}) copy-start(bf16[4,64,512]{2,1,0:T(8,128)(2,1)} %param.17) | copy-start | bytes 786436
  3.6 15.9 %all-to-all-start = ((bf16[8,4,512]{2,1,0:T(4,128)(2,1)}), bf16[8,4,512]{2,1,0:T(4,128)(2,1)S(1)}, u32[]{:S(2)}, u32[]{:S(2)}) async-start(bf16[8,4,512]{2,1,0:T(4,128)(2,1)} %broadcast_in_dim.55), calls=%async_computation | async-start | bytes 65536 | tf_op jit(solution)/shard_map/all_to_all | solution.py:56
  20.3 16.1 %all-to-all-start.1 = ((bf16[16,32,512]{2,1,0:T(8,128)(2,1)}), bf16[16,32,512]{2,1,0:T(8,128)(2,1)S(1)}, u32[]{:S(2)}, u32[]{:S(2)}) async-start(bf16[16,32,512]{2,1,0:T(8,128)(2,1)} %broadcast_in_dim.57), calls=%async_computation.1 | async-start | bytes 1048576 | tf_op jit(solution)/shard_map/all_to_all | solution.py:56
  27.1 17.6 %collective-permute-start = (bf16[32,1536]{1,0:T(8,128)(2,1)S(1)}, bf16[32,1536]{1,0:T(8,128)(2,1)S(1)}, u32[]{:S(2)}, u32[]{:S(2)}) collective-permute-start(bf16[32,1536]{1,0:T(8,128)(2,1)S(1)} %constant_dynamic-update-slice_fusion), channel_id=1, source_target_pairs={{0,1},{1,2},{2,3},{3,4},{4,5},{5,6},{6,7},{7,8},{8,9},{9,10},{10,1... | collective-permute-start | bytes 294920 | tf_op jit(solution)/shard_map/ppermute | solution.py:16
  34.4 10.3 %collective-permute-start.1 = (bf16[32,1536]{1,0:T(8,128)(2,1)S(1)}, bf16[32,1536]{1,0:T(8,128)(2,1)S(1)}, u32[]{:S(2)}, u32[]{:S(2)}) collective-permute-start(bf16[32,1536]{1,0:T(8,128)(2,1)S(1)} %constant_dynamic-update-slice_fusion), channel_id=1, source_target_pairs={{1,0},{2,1},{3,2},{4,3},{5,4},{6,5},{7,6},{8,7},{9,8},{10,9},{11,1... | collective-permute-start | bytes 294920 | tf_op jit(solution)/shard_map/ppermute | solution.py:19
  36.4 11.4 %collective-permute-start.2 = (bf16[512,512]{1,0:T(8,128)(2,1)S(1)}, bf16[512,512]{1,0:T(8,128)(2,1)}, u32[]{:S(2)}, u32[]{:S(2)}) collective-permute-start(bf16[512,512]{1,0:T(8,128)(2,1)S(1)} %bitcast.59), channel_id=1, source_target_pairs={{0,1},{1,0},{2,3},{3,2},{4,5},{5,4},{6,7},{7,6},{8,9},{9,8},{10,11... | collective-permute-start | bytes 1572872 | tf_op jit(solution)/shard_map/ppermute | solution.py:59
  48.9 4.3 %copy-start.1 = (bf16[24,8,8,128]{3,2,1,0:T(8,128)(2,1)S(1)}, bf16[24,8,8,128]{3,2,1,0:T(8,128)(2,1)}, u32[]{:S(2)}) copy-start(bf16[24,8,8,128]{3,2,1,0:T(8,128)(2,1)} %copy.30) | copy-start | bytes 1179652

commit v3 on v2

--- a/solution.py
+++ b/solution.py
@@ -19,6 +19,11 @@
         high = lax.ppermute(lax.slice_in_dim(block, 0, width, axis=dim), axis, backward)
         block = jnp.concatenate([low, block, high], axis=dim)
     return block
+
+
+def side_by_side(parts):
+    n, j, r, m = parts.shape
+    return parts.transpose(0, 2, 1, 3).reshape(n, r, j * m)
 
 
 def body(
@@ -43,10 +48,7 @@
     ).astype(jnp.bfloat16)
     children = skeleton.reshape(box_count, child_count, rhs_count, rank_width)
     coarse = jnp.einsum(
-        "ckim,cirm->crk",
-        transfer.reshape(box_count, rank_width, child_count, rank_width),
-        children,
-        preferred_element_type=jnp.float32,
+        "ckq,crq->crk", transfer, side_by_side(children), preferred_element_type=jnp.float32
     ).astype(jnp.bfloat16)
     coarse_flat = coarse.reshape(box_count, rhs_count * rank_width)
     everything = coarse_flat
@@ -76,10 +78,7 @@
         leaf_count, far_count, rhs_count, rank_width
     )
     leaf_far = jnp.einsum(
-        "lkjm,ljrm->lrk",
-        leaf_coupling.reshape(leaf_count, rank_width, far_count, rank_width),
-        far_skels,
-        preferred_element_type=jnp.float32,
+        "lkq,lrq->lrk", leaf_coupling, side_by_side(far_skels), preferred_element_type=jnp.float32
     )
     sizes = [lax.axis_size(a) for a in ALL]
     owner, slot = far_coarse // box_count, far_coarse % box_count
@@ -96,17 +95,16 @@
         box_count, coarse_count, rhs_count, rank_width
     )
     coarse_field = jnp.einsum(
-        "ckjm,cjrm->crk",
-        coarse_coupling.reshape(box_count, rank_width, coarse_count, rank_width),
-        coarse_skels,
-        preferred_element_type=jnp.float32,
+        "ckq,crq->crk", coarse_coupling, side_by_side(coarse_skels), preferred_element_type=jnp.float32
     ).astype(jnp.bfloat16)
     descended = jnp.einsum(
-        "ckim,crk->cirm",
-        transfer.reshape(box_count, rank_width, child_count, rank_width),
-        coarse_field,
-        preferred_element_type=jnp.float32,
-    ).reshape(leaf_count, rhs_count, rank_width)
+        "crk,ckq->crq", coarse_field, transfer, preferred_element_type=jnp.float32
+    )
+    descended = (
+        descended.reshape(box_count, rhs_count, child_count, rank_width)
+        .transpose(0, 2, 1, 3)
+        .reshape(leaf_count, rhs_count, rank_width)
+    )
     local_field = (leaf_far + descended).astype(jnp.bfloat16)
     total = (
         jnp.einsum("lrk,lkp->lrp", local_field, basis, preferred_element_type=jnp.float32)

time: 59 us -> 64.6 us (1.095)
  waiting for transfers between devices: 5.92 us -> 15.8 us
  local copies, waits for them, and re-layouts: 12.8 us -> 8.98 us
  starting transfers between devices: 28.1 us -> 25.1 us
  other arithmetic: 1.22 us -> 3.97 us
    all_to_all x2, waiting for transfers between devices: 5.91 us -> 15.8 us  [body(): lax.all_to_all(spread, axes, 0, 0, tiled=False)]
    reshape x3 -> x4, local copies, waits for them, and re-layouts: 5.76 us -> 0.65 us  [the longest x3 0.56 us: side_by_side(): return parts.transpose(0, 2, 1, 3).reshape(n, r, j * m)]
    ppermute x1, starting transfers between devices: 7.32 us -> 3.02 us  [with_halo(): lax.ppermute(lax.slice_in_dim(block, block.shape[dim] - width, None, axis...]
    ppermute x1, starting transfers between devices: 1.92 us -> 5.1 us  [with_halo(): lax.ppermute(lax.slice_in_dim(block, 0, width, axis=dim), axis, backward)]
    ppermute x1, starting transfers between devices: 3.07 us -> 0.01 us  [body(): partner = lax.ppermute(everything, PAIR, [(0, 1), (1, 0)])]
    dot_general x1, matrix products: 3.09 us -> 0.78 us  [body(): jnp.einsum('lrk,lkp->lrp', local_field, basis, preferred_element_type=jnp...]
    dot_general x2, matrix products: 0.72 us -> 2.35 us  [the longest x1 1.24 us: body(): jnp.einsum('crk,ckq->crq', coarse_field, transfer, preferred_element_type...]
    gather x2, local copies, waits for them, and re-layouts: 0.73 us -> 2.09 us  [body(): jnp.take(everything, position * box_count + slot, axis=0)]
  transfers between devices with their start and end apart: 5 -> 5, of which waited for: 1 -> 2; matrix products, arithmetic and copies ran while one was open for 16% -> 12% of each run, Pallas kernels for 0% -> 0%
where the time goes in v3:
time: 64.6 us; the launch traced here: 64 us
  starting transfers between devices  25.1 us (39%)
  waiting for transfers between devices  15.8 us (24%)
  matrix products  9.9 us (15%)
  local copies, waits for them, and re-layouts  8.98 us (14%)
  other arithmetic  3.97 us (6%)
    all_to_all x2, starting transfers between devices, body(): lax.all_to_all(spread, axes, 0, 0, tiled=False)  17 us
    all_to_all x2, waiting for transfers between devices, body(): lax.all_to_all(spread, axes, 0, 0, tiled=False)  15.8 us
    dot_general x1, matrix products, body(): jnp.einsum('ljpq,ljrq->lrp', near_blocks, near_rows, preferred_element_ty...  5.2 us
    ppermute x1, starting transfers between devices, with_halo(): lax.ppermute(lax.slice_in_dim(block, 0, width, axis=dim), axis, backward)  5.1 us
    ppermute x1, starting transfers between devices, with_halo(): lax.ppermute(lax.slice_in_dim(block, block.shape[dim] - width, None, axis...  3.02 us
    concatenate x1, other arithmetic, body(): everything = jnp.concatenate([everything, partner], axis=0)  2.14 us
    gather x2, local copies, waits for them, and re-layouts, body(): jnp.take(everything, position * box_count + slot, axis=0)  2.09 us
    broadcast_in_dim x4, local copies, waits for them, and re-layouts, body(): spread = jnp.broadcast_to(everything[None], (n,) + everything.shape)  1.6 us
  transfers between devices with their start and end apart: 5, of which 2 were waited for; matrix products, arithmetic and copies ran while one was open for 12% of the time, Pallas kernels for 0%

profile of v3, /device:TPU:1, one launch (start us, length us, event | category | flops | bytes accessed | tf_op | source)
XLA Modules:
  0.0 64.0 jit_solution(17456498739737645226)
XLA Ops:
  0.0 1.6 %convolution_convert_fusion = bf16[32,8,64]{2,1,0:T(8,128)(2,1)S(1)} fusion(bf16[32,8,128]{2,1,0:T(8,128)(2,1)} %param.9, bf16[32,64,128]{2,1,0:T(8,128)(2,1)} %param.10), kind=kOutput, calls=%fused_computation.8 | convolution fusion | flops 4210688 | bytes 622592 | tf_op jit(solution)/shard_map/lrp,lkp->lrk/dot_general | solution.py:46
  1.6 0.9 %bitcast_dynamic-update-slice_fusion = bf16[32,1536]{1,0:T(8,128)(2,1)S(1)} fusion(bf16[4,8,8,128]{3,2,1,0:T(8,128)(2,1)} %bitcast.45), kind=kLoop, calls=%fused_computation.22 | loop fusion | bytes 131072
  2.6 5.1 %collective-permute-start.1 = (bf16[32,1536]{1,0:T(8,128)(2,1)S(1)}, bf16[32,1536]{1,0:T(8,128)(2,1)S(1)}, u32[]{:S(2)}, u32[]{:S(2)}) collective-permute-start(bf16[32,1536]{1,0:T(8,128)(2,1)S(1)} %constant_dynamic-update-slice_fusion), channel_id=1, source_target_pairs={{1,0},{2,1},{3,2},{4,3},{5,4},{6,5},{7,6},{8,7},{9,8},{10,9},{11,1... | collective-permute-start | bytes 294920 | tf_op jit(solution)/shard_map/ppermute | solution.py:19
  7.7 3.0 %collective-permute-start = (bf16[32,1536]{1,0:T(8,128)(2,1)S(1)}, bf16[32,1536]{1,0:T(8,128)(2,1)S(1)}, u32[]{:S(2)}, u32[]{:S(2)}) collective-permute-start(bf16[32,1536]{1,0:T(8,128)(2,1)S(1)} %constant_dynamic-update-slice_fusion), channel_id=1, source_target_pairs={{0,1},{1,2},{2,3},{3,4},{4,5},{5,6},{6,7},{7,8},{8,9},{9,10},{10,1... | collective-permute-start | bytes 294920 | tf_op jit(solution)/shard_map/ppermute | solution.py:16
  10.8 1.1 %convolution_convert_fusion.2 = bf16[4,8,64]{2,1,0:T(8,128)(2,1)S(1)} fusion(bf16[4,8,512]{2,1,0:T(8,128)(2,1)S(1)} %reshape.54, bf16[4,64,512]{2,1,0:T(8,128)(2,1)} %param.15), kind=kOutput, calls=%fused_computation.11 | convolution fusion | flops 2099200 | bytes 299008 | tf_op jit(solution)/shard_map/ckq,crq->crk/dot_general | solution.py:50
  12.1 0.6 %broadcast_in_dim.55 = bf16[8,4,512]{2,1,0:T(4,128)(2,1)} broadcast(bf16[4,512]{1,0:T(4,128)(2,1)S(1)} %broadcast_in_dim.54), dimensions={1,2} | broadcast | bytes 36864 | tf_op jit(solution)/shard_map/broadcast_in_dim | solution.py:57
  12.7 8.2 %all-to-all-start = ((bf16[8,4,512]{2,1,0:T(4,128)(2,1)}), bf16[8,4,512]{2,1,0:T(4,128)(2,1)S(1)}, u32[]{:S(2)}, u32[]{:S(2)}) async-start(bf16[8,4,512]{2,1,0:T(4,128)(2,1)} %broadcast_in_dim.55), calls=%async_computation | async-start | bytes 65536 | tf_op jit(solution)/shard_map/all_to_all | solution.py:58
  20.9 0.7 %compare_and_fusion.2 = (pred[4,8]{1,0:T(4,128)(4,1)S(1)}, s32[4,8]{1,0:T(4,128)S(1)}) fusion(s32[]{:T(128)S(6)} %axis_index.56, s32[4,8]{1,0:T(4,128)} %param.16), kind=kLoop, calls=%fused_computation.82 | loop fusion | flops 3936 | bytes 292 | tf_op jit(solution)/shard_map/jit(_take)/and | solution.py:94
  21.7 6.1 %all-to-all-done = bf16[8,4,512]{2,1,0:T(4,128)(2,1)S(1)} async-done(((bf16[8,4,512]{2,1,0:T(4,128)(2,1)}), bf16[8,4,512]{2,1,0:T(4,128)(2,1)S(1)}, u32[]{:S(2)}, u32[]{:S(2)}) %all-to-all-start) | async-done | bytes 32800 | tf_op jit(solution)/shard_map/all_to_all | solution.py:58
  27.8 0.8 %broadcast_in_dim.57 = bf16[16,32,512]{2,1,0:T(8,128)(2,1)} broadcast(bf16[32,512]{1,0:T(8,128)(2,1)S(1)} %broadcast_in_dim.56), dimensions={1,2} | broadcast | bytes 557056 | tf_op jit(solution)/shard_map/broadcast_in_dim | solution.py:57
  28.6 8.8 %all-to-all-start.1 = ((bf16[16,32,512]{2,1,0:T(8,128)(2,1)}), bf16[16,32,512]{2,1,0:T(8,128)(2,1)S(1)}, u32[]{:S(2)}, u32[]{:S(2)}) async-start(bf16[16,32,512]{2,1,0:T(8,128)(2,1)} %broadcast_in_dim.57), calls=%async_computation.1 | async-start | bytes 1048576 | tf_op jit(solution)/shard_map/all_to_all | solution.py:58
  37.9 9.7 %all-to-all-done.1 = bf16[16,32,512]{2,1,0:T(8,128)(2,1)S(1)} async-done(((bf16[16,32,512]{2,1,0:T(8,128)(2,1)}), bf16[16,32,512]{2,1,0:T(8,128)(2,1)S(1)}, u32[]{:S(2)}, u32[]{:S(2)}) %all-to-all-start.1) | async-done | bytes 524320 | tf_op jit(solution)/shard_map/all_to_all | solution.py:58
  47.9 0.6 copy-done.3
  48.5 1.0 %gather_fusion = bf16[192,512]{1,0:T(8,128)(2,1)S(1)} fusion(bf16[96,512]{1,0:T(8,128)(2,1)S(1)} %pad_maximum_fusion.3, s32[1024]{0:T(1024)S(1)} %get-tuple-element.12), kind=kCustom, calls=%fused_computation | custom fusion | bytes 393984 | tf_op jit(solution)/shard_map/jit(_take)/gather | solution.py:77
  49.5 0.2 gather.19
  49.8 0.3 reshape.52
  50.2 0.9 %pad_maximum_fusion.1 = bf16[96,1024]{1,0:T(8,128)(2,1)S(1)} fusion(bf16[32,1536]{1,0:T(8,128)(2,1)S(1)} %collective-permute-done.1, bf16[32,1536]{1,0:T(8,128)(2,1)S(1)} %constant_dynamic-update-slice_fusion, bf16[32,1536]{1,0:T(8,128)(2,1)} %copy-done.3), kind=kLoop, calls=%fused_computation.18 | loop fusion | flops 589824 | bytes 491520 | tf_op jit(solution)/shard_map/concatenate | solution.py:20
  51.0 1.0 %gather_fusion.2 = bf16[192,1024]{1,0:T(8,128)(2,1)S(1)} fusion(bf16[96,1024]{1,0:T(8,128)(2,1)S(1)} %pad_maximum_fusion.1, s32[1024]{0:T(1024)S(1)} %get-tuple-element.11), kind=kCustom, calls=%fused_computation.2 | custom fusion | bytes 787200 | tf_op jit(solution)/shard_map/jit(_take)/gather | solution.py:71
  52.1 2.1 %pad_maximum_fusion = bf16[1024,512]{1,0:T(8,128)(2,1)} fusion(bf16[512,512]{1,0:T(8,128)(2,1)} %collective-permute-done.2, bf16[512,512]{1,0:T(8,128)(2,1)S(1)} %bitcast.40), kind=kLoop, calls=%fused_computation.13 | loop fusion | flops 2097152 | bytes 2097152 | tf_op jit(solution)/shard_map/concatenate | solution.py:62
  54.3 2.0 %gather_fusion.1 = bf16[32,512]{1,0:T(8,128)(2,1)S(1)} fusion(bf16[1024,512]{1,0:T(8,128)(2,1)} %pad_maximum_fusion, s32[1024]{0:T(1024)S(1)} %pad_clamp_fusion.1), kind=kCustom, calls=%fused_computation.1 | custom fusion | bytes 65664 | tf_op jit(solution)/shard_map/jit(_take)/gather | solution.py:94
  56.5 0.1 reshape.56
  56.6 1.2 %fusion.4 = f32[4,8,512]{2,1,0:T(8,128)S(1)} fusion(bf16[4,64,512]{2,1,0:T(8,128)(2,1)S(1)} %copy-done.2, bf16[4,8,512]{2,1,0:T(8,128)(2,1)S(1)} %reshape.56, bf16[4,64,512]{2,1,0:T(8,128)(2,1)} %param.17), kind=kOutput, calls=%fused_computation.12 | convolution fusion | flops 4196352 | bytes 622592 | tf_op jit(solution)/shard_map/crk,ckq->crq/dot_general | solution.py:100
  58.0 0.8 %fusion.3 = f32[32,8,128]{2,1,0:T(8,128)S(1)} fusion(bf16[32,64,128]{2,1,0:T(8,128)(2,1)S(1)} %copy-done.1, f32[32,8,64]{2,1,0:T(8,128)S(1)} %bitcast.43, bf16[32,8,384]{2,1,0:T(8,128)(2,1)S(1)} %reshape.52, bf16[32,64,384]{2,1,0:T(8,128)(2,1)S(1)} %copy-done), kind=kOutput, calls=%fused_computation.9 | convolution fusion | flops 16809984 | bytes 2490368 | tf_op jit(solution)/shard_map/lrk,lkp->lrp/dot_general | solution.py:110
  58.8 5.2 %fusion.2 = bf16[32,8,128]{2,1,0:T(8,128)(2,1)} fusion(f32[32,8,128]{2,1,0:T(8,128)S(1)} %fusion.3, bf16[32,6,128,128]{3,2,1,0:T(8,128)(2,1)} %param.12, bf16[32,6,8,128]{3,2,1,0:T(8,128)(2,1)S(1)} %bitcast.41, pred[32,6]{1,0:T(8,128)(4,1)S(1)} %copy.20), kind=kOutput, calls=%fused_computation.7 | convolution fusion | flops 50593792 | bytes 6881472 | tf_op jit(solution)/shard_map/ljpq,ljrq->lrp/dot_general | solution.py:74
  (39 shorter events, 1.6 us)
Async XLA Ops:
  0.0 58.0 %copy-start = (bf16[32,64,384]{2,1,0:T(8,128)(2,1)S(1)}, bf16[32,64,384]{2,1,0:T(8,128)(2,1)}, u32[]{:S(2)}) copy-start(bf16[32,64,384]{2,1,0:T(8,128)(2,1)} %param.14) | copy-start | bytes 4718596
  0.0 37.4 %copy-start.4 = (s32[32,6]{0,1:T(8,128)S(1)}, s32[32,6]{0,1:T(8,128)}, u32[]{:S(2)}) copy-start(s32[32,6]{0,1:T(8,128)} %param.11) | copy-start | bytes 2308
  0.0 37.6 %copy-start.5 = (s32[32,6]{0,1:T(8,128)S(1)}, s32[32,6]{0,1:T(8,128)}, u32[]{:S(2)}) copy-start(s32[32,6]{0,1:T(8,128)} %param.13) | copy-start | bytes 2308
  2.6 45.3 %collective-permute-start.1 = (bf16[32,1536]{1,0:T(8,128)(2,1)S(1)}, bf16[32,1536]{1,0:T(8,128)(2,1)S(1)}, u32[]{:S(2)}, u32[]{:S(2)}) collective-permute-start(bf16[32,1536]{1,0:T(8,128)(2,1)S(1)} %constant_dynamic-update-slice_fusion), channel_id=1, source_target_pairs={{1,0},{2,1},{3,2},{4,3},{5,4},{6,5},{7,6},{8,7},{9,8},{10,9},{11,1... | collective-permute-start | bytes 294920 | tf_op jit(solution)/shard_map/ppermute | solution.py:19
  7.7 40.2 %collective-permute-start = (bf16[32,1536]{1,0:T(8,128)(2,1)S(1)}, bf16[32,1536]{1,0:T(8,128)(2,1)S(1)}, u32[]{:S(2)}, u32[]{:S(2)}) collective-permute-start(bf16[32,1536]{1,0:T(8,128)(2,1)S(1)} %constant_dynamic-update-slice_fusion), channel_id=1, source_target_pairs={{0,1},{1,2},{2,3},{3,4},{4,5},{5,6},{6,7},{7,8},{8,9},{9,10},{10,1... | collective-permute-start | bytes 294920 | tf_op jit(solution)/shard_map/ppermute | solution.py:16
  12.7 15.1 %all-to-all-start = ((bf16[8,4,512]{2,1,0:T(4,128)(2,1)}), bf16[8,4,512]{2,1,0:T(4,128)(2,1)S(1)}, u32[]{:S(2)}, u32[]{:S(2)}) async-start(bf16[8,4,512]{2,1,0:T(4,128)(2,1)} %broadcast_in_dim.55), calls=%async_computation | async-start | bytes 65536 | tf_op jit(solution)/shard_map/all_to_all | solution.py:58
  28.6 19.0 %all-to-all-start.1 = ((bf16[16,32,512]{2,1,0:T(8,128)(2,1)}), bf16[16,32,512]{2,1,0:T(8,128)(2,1)S(1)}, u32[]{:S(2)}, u32[]{:S(2)}) async-start(bf16[16,32,512]{2,1,0:T(8,128)(2,1)} %broadcast_in_dim.57), calls=%async_computation.1 | async-start | bytes 1048576 | tf_op jit(solution)/shard_map/all_to_all | solution.py:58
  47.6 4.5 %collective-permute-start.2 = (bf16[512,512]{1,0:T(8,128)(2,1)S(1)}, bf16[512,512]{1,0:T(8,128)(2,1)}, u32[]{:S(2)}, u32[]{:S(2)}) collective-permute-start(bf16[512,512]{1,0:T(8,128)(2,1)S(1)} %bitcast.39), channel_id=1, source_target_pairs={{0,1},{1,0},{2,3},{3,2},{4,5},{5,4},{6,7},{7,6},{8,9},{9,8},{10,11... | collective-permute-start | bytes 1572872 | tf_op jit(solution)/shard_map/ppermute | solution.py:61
  47.8 0.6 %copy-start.3 = (bf16[32,1536]{1,0:T(8,128)(2,1)}, bf16[32,1536]{1,0:T(8,128)(2,1)S(1)}, u32[]{:S(2)}) copy-start(bf16[32,1536]{1,0:T(8,128)(2,1)S(1)} %collective-permute-done) | copy-start | bytes 294916
  52.0 4.5 %copy-start.2 = (bf16[4,64,512]{2,1,0:T(8,128)(2,1)S(1)}, bf16[4,64,512]{2,1,0:T(8,128)(2,1)}, u32[]{:S(2)}) copy-start(bf16[4,64,512]{2,1,0:T(8,128)(2,1)} %param.15) | copy-start | bytes 786436
  52.1 5.9 %copy-start.1 = (bf16[32,64,128]{2,1,0:T(8,128)(2,1)S(1)}, bf16[32,64,128]{2,1,0:T(8,128)(2,1)}, u32[]{:S(2)}) copy-start(bf16[32,64,128]{2,1,0:T(8,128)(2,1)} %param.10) | copy-start | bytes 1572868

commit v4 on v3

--- a/solution.py
+++ b/solution.py
@@ -80,6 +80,7 @@
     leaf_far = jnp.einsum(
         "lkq,lrq->lrk", leaf_coupling, side_by_side(far_skels), preferred_element_type=jnp.float32
     )
+    near_part, leaf_far = lax.optimization_barrier((near_part, leaf_far))
     sizes = [lax.axis_size(a) for a in ALL]
     owner, slot = far_coarse // box_count, far_coarse % box_count
     coords = []

time: 64.6 us -> 59.7 us (0.924)
  waiting for transfers between devices: 15.8 us -> 12.6 us
  matrix products: 9.9 us -> 8.92 us
    all_to_all x2, waiting for transfers between devices: 15.8 us -> 12.5 us  [body(): lax.all_to_all(spread, axes, 0, 0, tiled=False)]
    dot_general x1, matrix products: 1.24 us -> 0.29 us  [body(): jnp.einsum('crk,ckq->crq', coarse_field, transfer, preferred_element_type...]
    concatenate x1, other arithmetic: 0.85 us -> 0.02 us  [with_halo(): block = jnp.concatenate([low, block, high], axis=dim)]
    and x1, other arithmetic: 0.01 us -> 0.71 us  [body(): jnp.take(skeleton_padded, far_leaf - offset_base, axis=0)]
    dot_general x1, matrix products: 5.2 us -> 4.55 us  [body(): jnp.einsum('ljpq,ljrq->lrp', near_blocks, near_rows, preferred_element_ty...]
    unnamed x14 -> x10, local copies, waits for them, and re-layouts: 1.57 us -> 1.05 us
  transfers between devices with their start and end apart: 5 -> 5, of which waited for: 2 -> 2; matrix products, arithmetic and copies ran while one was open for 12% -> 22% of each run, Pallas kernels for 0% -> 0%
where the time goes in v4:
time: 59.7 us; the launch traced here: 59.2 us
  starting transfers between devices  25.1 us (42%)
  waiting for transfers between devices  12.6 us (21%)
  matrix products  8.92 us (15%)
  local copies, waits for them, and re-layouts  8.5 us (14%)
  other arithmetic  3.88 us (6%)
    all_to_all x2, starting transfers between devices, body(): lax.all_to_all(spread, axes, 0, 0, tiled=False)  17 us
    all_to_all x2, waiting for transfers between devices, body(): lax.all_to_all(spread, axes, 0, 0, tiled=False)  12.5 us
    ppermute x1, starting transfers between devices, with_halo(): lax.ppermute(lax.slice_in_dim(block, 0, width, axis=dim), axis, backward)  5.11 us
    dot_general x1, matrix products, body(): jnp.einsum('ljpq,ljrq->lrp', near_blocks, near_rows, preferred_element_ty...  4.55 us
    ppermute x1, starting transfers between devices, with_halo(): lax.ppermute(lax.slice_in_dim(block, block.shape[dim] - width, None, axis...  3.01 us
    concatenate x1, other arithmetic, body(): everything = jnp.concatenate([everything, partner], axis=0)  2.17 us
    gather x2, local copies, waits for them, and re-layouts, body(): jnp.take(everything, position * box_count + slot, axis=0)  2.09 us
    broadcast_in_dim x4, local copies, waits for them, and re-layouts, body(): spread = jnp.broadcast_to(everything[None], (n,) + everything.shape)  1.61 us
  transfers between devices with their start and end apart: 5, of which 2 were waited for; matrix products, arithmetic and copies ran while one was open for 22% of the time, Pallas kernels for 0%

profile of v4, /device:TPU:1, one launch (start us, length us, event | category | flops | bytes accessed | tf_op | source)
XLA Modules:
  0.0 59.2 jit_solution(14236201596378656979)
XLA Ops:
  0.0 1.0 %bitcast_dynamic-update-slice_fusion = bf16[32,1536]{1,0:T(8,128)(2,1)S(1)} fusion(bf16[4,8,8,128]{3,2,1,0:T(8,128)(2,1)} %bitcast.44), kind=kLoop, calls=%fused_computation.20 | loop fusion | bytes 131072
  1.0 1.4 %convolution_convert_fusion = bf16[32,8,64]{2,1,0:T(8,128)(2,1)S(1)} fusion(bf16[32,8,128]{2,1,0:T(8,128)(2,1)} %param.9, bf16[32,64,128]{2,1,0:T(8,128)(2,1)} %param.10), kind=kOutput, calls=%fused_computation.6 | convolution fusion | flops 4210688 | bytes 622592 | tf_op jit(solution)/shard_map/lrp,lkp->lrk/dot_general | solution.py:46
  2.4 0.1 reshape.51
  2.6 5.1 %collective-permute-start.1 = (bf16[32,1536]{1,0:T(8,128)(2,1)S(1)}, bf16[32,1536]{1,0:T(8,128)(2,1)S(1)}, u32[]{:S(2)}, u32[]{:S(2)}) collective-permute-start(bf16[32,1536]{1,0:T(8,128)(2,1)S(1)} %constant_dynamic-update-slice_fusion), channel_id=1, source_target_pairs={{1,0},{2,1},{3,2},{4,3},{5,4},{6,5},{7,6},{8,7},{9,8},{10,9},{11,1... | collective-permute-start | bytes 294920 | tf_op jit(solution)/shard_map/ppermute | solution.py:19
  7.7 3.0 %collective-permute-start = (bf16[32,1536]{1,0:T(8,128)(2,1)S(1)}, bf16[32,1536]{1,0:T(8,128)(2,1)S(1)}, u32[]{:S(2)}, u32[]{:S(2)}) collective-permute-start(bf16[32,1536]{1,0:T(8,128)(2,1)S(1)} %constant_dynamic-update-slice_fusion), channel_id=1, source_target_pairs={{0,1},{1,2},{2,3},{3,4},{4,5},{5,6},{6,7},{7,8},{8,9},{9,10},{10,1... | collective-permute-start | bytes 294920 | tf_op jit(solution)/shard_map/ppermute | solution.py:16
  10.8 1.1 %convolution_convert_fusion.2 = bf16[4,8,64]{2,1,0:T(8,128)(2,1)S(1)} fusion(bf16[4,8,512]{2,1,0:T(8,128)(2,1)S(1)} %reshape.54, bf16[4,64,512]{2,1,0:T(8,128)(2,1)} %param.15), kind=kOutput, calls=%fused_computation.8 | convolution fusion | flops 2099200 | bytes 299008 | tf_op jit(solution)/shard_map/ckq,crq->crk/dot_general | solution.py:50
  12.1 0.6 %broadcast_in_dim.58 = bf16[8,4,512]{2,1,0:T(4,128)(2,1)} broadcast(bf16[4,512]{1,0:T(4,128)(2,1)S(1)} %broadcast_in_dim.57), dimensions={1,2} | broadcast | bytes 36864 | tf_op jit(solution)/shard_map/broadcast_in_dim | solution.py:57
  12.7 8.2 %all-to-all-start = ((bf16[8,4,512]{2,1,0:T(4,128)(2,1)}), bf16[8,4,512]{2,1,0:T(4,128)(2,1)S(1)}, u32[]{:S(2)}, u32[]{:S(2)}) async-start(bf16[8,4,512]{2,1,0:T(4,128)(2,1)} %broadcast_in_dim.58), calls=%async_computation | async-start | bytes 65536 | tf_op jit(solution)/shard_map/all_to_all | solution.py:58
  20.9 0.7 %compare_and_fusion = (pred[32,6]{0,1:T(8,128)(4,1)S(1)}, s32[32,6]{0,1:T(8,128)S(1)}, pred[32,6]{0,1:T(8,128)(4,1)S(1)}, s32[32,6]{0,1:T(8,128)S(1)}) fusion(s32[32,6]{0,1:T(8,128)} %param.13, s32[]{:T(128)S(6)} %sub.35, s32[32,6]{0,1:T(8,128)} %param.11), kind=kLoop, calls=%fused_computation.30 | loop fusion | flops 2688 | bytes 3460 | tf_op jit(solution)/shard_map/jit(_take)/and | solution.py:77
  22.2 0.7 %compare_and_fusion.2 = (pred[4,8]{1,0:T(4,128)(4,1)S(1)}, s32[4,8]{1,0:T(4,128)S(1)}) fusion(s32[]{:T(128)S(6)} %axis_index.56, s32[4,8]{1,0:T(4,128)} %param.16), kind=kLoop, calls=%fused_computation.80 | loop fusion | flops 3936 | bytes 292 | tf_op jit(solution)/shard_map/jit(_take)/and | solution.py:95
  23.0 4.7 %all-to-all-done = bf16[8,4,512]{2,1,0:T(4,128)(2,1)S(1)} async-done(((bf16[8,4,512]{2,1,0:T(4,128)(2,1)}), bf16[8,4,512]{2,1,0:T(4,128)(2,1)S(1)}, u32[]{:S(2)}, u32[]{:S(2)}) %all-to-all-start) | async-done | bytes 32800 | tf_op jit(solution)/shard_map/all_to_all | solution.py:58
  27.8 0.9 %broadcast_in_dim.60 = bf16[16,32,512]{2,1,0:T(8,128)(2,1)} broadcast(bf16[32,512]{1,0:T(8,128)(2,1)S(1)} %broadcast_in_dim.59), dimensions={1,2} | broadcast | bytes 557056 | tf_op jit(solution)/shard_map/broadcast_in_dim | solution.py:57
  28.6 8.8 %all-to-all-start.1 = ((bf16[16,32,512]{2,1,0:T(8,128)(2,1)}), bf16[16,32,512]{2,1,0:T(8,128)(2,1)S(1)}, u32[]{:S(2)}, u32[]{:S(2)}) async-start(bf16[16,32,512]{2,1,0:T(8,128)(2,1)} %broadcast_in_dim.60), calls=%async_computation.1 | async-start | bytes 1048576 | tf_op jit(solution)/shard_map/all_to_all | solution.py:58
  37.5 1.0 %gather_fusion.1 = bf16[192,512]{1,0:T(8,128)(2,1)S(1)} fusion(bf16[96,512]{1,0:T(8,128)(2,1)S(1)} %pad_maximum_fusion.2, s32[1024]{0:T(1024)S(1)} %pad_clamp_fusion.1), kind=kCustom, calls=%fused_computation.1 | custom fusion | bytes 393984 | tf_op jit(solution)/shard_map/jit(_take)/gather | solution.py:77
  38.5 0.2 gather.21
  38.8 0.3 reshape.52
  39.2 0.6 %fusion.26 = f32[32,8,64]{2,1,0:T(8,128)S(1)} fusion(bf16[32,8,384]{2,1,0:T(8,128)(2,1)S(1)} %reshape.52, bf16[32,64,384]{2,1,0:T(8,128)(2,1)S(1)} %copy-done), kind=kOutput, calls=%fused_computation.84 | convolution fusion | flops 12582912 | bytes 1835008 | tf_op jit(solution)/shard_map/lkq,lrq->lrk/dot_general | solution.py:80
  39.8 7.8 %all-to-all-done.1 = bf16[16,32,512]{2,1,0:T(8,128)(2,1)S(1)} async-done(((bf16[16,32,512]{2,1,0:T(8,128)(2,1)}), bf16[16,32,512]{2,1,0:T(8,128)(2,1)S(1)}, u32[]{:S(2)}, u32[]{:S(2)}) %all-to-all-start.1) | async-done | bytes 524320 | tf_op jit(solution)/shard_map/all_to_all | solution.py:58
  47.7 1.0 %gather_fusion = bf16[192,1024]{1,0:T(8,128)(2,1)S(1)} fusion(bf16[96,1024]{1,0:T(8,128)(2,1)S(1)} %slice.14, s32[1024]{0:T(1024)S(1)} %pad_clamp_fusion.2), kind=kCustom, calls=%fused_computation | custom fusion | bytes 787200 | tf_op jit(solution)/shard_map/jit(_take)/gather | solution.py:71
  48.8 4.5 %convolution_bitcast_fusion = f32[32,8,128]{2,1,0:T(8,128)S(1)} fusion(bf16[32,6,128,128]{3,2,1,0:T(8,128)(2,1)} %param.12, bf16[32,6,8,128]{3,2,1,0:T(8,128)(2,1)S(1)} %bitcast.42, pred[32,6]{1,0:T(8,128)(4,1)S(1)} %copy.15), kind=kOutput, calls=%fused_computation.4 | convolution fusion | flops 50528256 | bytes 6815936 | tf_op jit(solution)/shard_map/ljpq,ljrq->lrp/dot_general | solution.py:74
  53.3 2.2 %pad_maximum_fusion = bf16[1024,512]{1,0:T(8,128)(2,1)} fusion(bf16[512,512]{1,0:T(8,128)(2,1)} %collective-permute-done.2, bf16[512,512]{1,0:T(8,128)(2,1)S(1)} %bitcast.41), kind=kLoop, calls=%fused_computation.10 | loop fusion | flops 2097152 | bytes 2097152 | tf_op jit(solution)/shard_map/concatenate | solution.py:62
  55.5 2.0 %gather_fusion.2 = bf16[32,512]{1,0:T(8,128)(2,1)S(1)} fusion(bf16[1024,512]{1,0:T(8,128)(2,1)} %pad_maximum_fusion, s32[1024]{0:T(1024)S(1)} %pad_clamp_fusion), kind=kCustom, calls=%fused_computation.2 | custom fusion | bytes 65664 | tf_op jit(solution)/shard_map/jit(_take)/gather | solution.py:95
  57.8 0.3 fusion.1
  58.3 0.9 %fusion = bf16[32,8,128]{2,1,0:T(8,128)(2,1)} fusion(f32[32,8,128]{2,1,0:T(8,128)S(1)} %convolution_bitcast_fusion, bf16[32,8,64]{2,1,0:T(8,128)(2,1)S(1)} %fusion.6, bf16[32,64,128]{2,1,0:T(8,128)(2,1)S(1)} %copy-done.1), kind=kOutput, calls=%fused_computation.5 | convolution fusion | flops 4259840 | bytes 753664 | tf_op jit(solution)/shard_map/lrk,lkp->lrp/dot_general | solution.py:111
  (38 shorter events, 1.6 us)
Async XLA Ops:
  0.0 39.2 %copy-start = (bf16[32,64,384]{2,1,0:T(8,128)(2,1)S(1)}, bf16[32,64,384]{2,1,0:T(8,128)(2,1)}, u32[]{:S(2)}) copy-start(bf16[32,64,384]{2,1,0:T(8,128)(2,1)} %param.14) | copy-start | bytes 4718596
  2.6 34.9 %collective-permute-start.1 = (bf16[32,1536]{1,0:T(8,128)(2,1)S(1)}, bf16[32,1536]{1,0:T(8,128)(2,1)S(1)}, u32[]{:S(2)}, u32[]{:S(2)}) collective-permute-start(bf16[32,1536]{1,0:T(8,128)(2,1)S(1)} %constant_dynamic-update-slice_fusion), channel_id=1, source_target_pairs={{1,0},{2,1},{3,2},{4,3},{5,4},{6,5},{7,6},{8,7},{9,8},{10,9},{11,1... | collective-permute-start | bytes 294920 | tf_op jit(solution)/shard_map/ppermute | solution.py:19
  7.7 29.8 %collective-permute-start = (bf16[32,1536]{1,0:T(8,128)(2,1)S(1)}, bf16[32,1536]{1,0:T(8,128)(2,1)S(1)}, u32[]{:S(2)}, u32[]{:S(2)}) collective-permute-start(bf16[32,1536]{1,0:T(8,128)(2,1)S(1)} %constant_dynamic-update-slice_fusion), channel_id=1, source_target_pairs={{0,1},{1,2},{2,3},{3,4},{4,5},{5,6},{6,7},{7,8},{8,9},{9,10},{10,1... | collective-permute-start | bytes 294920 | tf_op jit(solution)/shard_map/ppermute | solution.py:16
  12.7 15.1 %all-to-all-start = ((bf16[8,4,512]{2,1,0:T(4,128)(2,1)}), bf16[8,4,512]{2,1,0:T(4,128)(2,1)S(1)}, u32[]{:S(2)}, u32[]{:S(2)}) async-start(bf16[8,4,512]{2,1,0:T(4,128)(2,1)} %broadcast_in_dim.58), calls=%async_computation | async-start | bytes 65536 | tf_op jit(solution)/shard_map/all_to_all | solution.py:58
  28.6 19.0 %all-to-all-start.1 = ((bf16[16,32,512]{2,1,0:T(8,128)(2,1)}), bf16[16,32,512]{2,1,0:T(8,128)(2,1)S(1)}, u32[]{:S(2)}, u32[]{:S(2)}) async-start(bf16[16,32,512]{2,1,0:T(8,128)(2,1)} %broadcast_in_dim.60), calls=%async_computation.1 | async-start | bytes 1048576 | tf_op jit(solution)/shard_map/all_to_all | solution.py:58
  47.6 5.7 %collective-permute-start.2 = (bf16[512,512]{1,0:T(8,128)(2,1)S(1)}, bf16[512,512]{1,0:T(8,128)(2,1)}, u32[]{:S(2)}, u32[]{:S(2)}) collective-permute-start(bf16[512,512]{1,0:T(8,128)(2,1)S(1)} %bitcast.40), channel_id=1, source_target_pairs={{0,1},{1,0},{2,3},{3,2},{4,5},{5,4},{6,7},{7,6},{8,9},{9,8},{10,11... | collective-permute-start | bytes 1572872 | tf_op jit(solution)/shard_map/ppermute | solution.py:61
  53.3 4.5 %copy-start.2 = (bf16[4,64,512]{2,1,0:T(8,128)(2,1)S(1)}, bf16[4,64,512]{2,1,0:T(8,128)(2,1)}, u32[]{:S(2)}) copy-start(bf16[4,64,512]{2,1,0:T(8,128)(2,1)} %param.15) | copy-start | bytes 786436
  53.3 4.5 %copy-start.3 = (bf16[4,64,512]{2,1,0:T(8,128)(2,1)S(1)}, bf16[4,64,512]{2,1,0:T(8,128)(2,1)}, u32[]{:S(2)}) copy-start(bf16[4,64,512]{2,1,0:T(8,128)(2,1)} %param.17) | copy-start | bytes 786436
  53.3 5.0 %copy-start.1 = (bf16[32,64,128]{2,1,0:T(8,128)(2,1)S(1)}, bf16[32,64,128]{2,1,0:T(8,128)(2,1)}, u32[]{:S(2)}) copy-start(bf16[32,64,128]{2,1,0:T(8,128)(2,1)} %param.10) | copy-start | bytes 1572868

commit v5 on v3

--- a/solution.py
+++ b/solution.py
@@ -58,8 +58,6 @@
         everything = lax.all_to_all(spread, axes, 0, 0, tiled=False).reshape(
             (n * everything.shape[0],) + everything.shape[1:]
         )
-    partner = lax.ppermute(everything, PAIR, [(0, 1), (1, 0)])
-    everything = jnp.concatenate([everything, partner], axis=0)
     offset_base = lax.axis_index(ALL) * leaf_count - leaf_count
     density_flat = density.reshape(leaf_count, rhs_count * leaf_width)
     skeleton_flat = skeleton.reshape(leaf_count, rhs_count * rank_width)
@@ -80,6 +78,8 @@
     leaf_far = jnp.einsum(
         "lkq,lrq->lrk", leaf_coupling, side_by_side(far_skels), preferred_element_type=jnp.float32
     )
+    everything, near_part, leaf_far = lax.optimization_barrier((everything, near_part, leaf_far))
+    partner = lax.ppermute(everything, PAIR, [(0, 1), (1, 0)])
     sizes = [lax.axis_size(a) for a in ALL]
     owner, slot = far_coarse // box_count, far_coarse % box_count
     coords = []
@@ -87,13 +87,16 @@
         coords.append(owner % size)
         owner = owner // size
     coords = dict(zip(reversed(ALL), coords))
-    position = (coords[PAIR] != lax.axis_index(PAIR)).astype(jnp.int32)
+    position = 0
     for axes in reversed(STAGES):
         for a in axes:
             position = position * lax.axis_size(a) + coords[a]
-    coarse_skels = jnp.take(everything, position * box_count + slot, axis=0).reshape(
-        box_count, coarse_count, rhs_count, rank_width
-    )
+    row = position * box_count + slot
+    coarse_skels = jnp.where(
+        (coords[PAIR] != lax.axis_index(PAIR))[:, :, None],
+        jnp.take(partner, row, axis=0),
+        jnp.take(everything, row, axis=0),
+    ).reshape(box_count, coarse_count, rhs_count, rank_width)
     coarse_field = jnp.einsum(
         "ckq,crq->crk", coarse_coupling, side_by_side(coarse_skels), preferred_element_type=jnp.float32
     ).astype(jnp.bfloat16)

time: 64.6 us -> 53.5 us (0.83)
  waiting for transfers between devices: 15.8 us -> 6.5 us
  other arithmetic: 3.97 us -> 1.03 us
  starting transfers between devices: 25.1 us -> 26.8 us
    all_to_all x2, waiting for transfers between devices: 15.8 us -> 5.61 us  [body(): lax.all_to_all(spread, axes, 0, 0, tiled=False)]
    ppermute x1, starting transfers between devices: 0.01 us -> 6.21 us  [body(): partner = lax.ppermute(everything, PAIR, [(0, 1), (1, 0)])]
    all_to_all x2, starting transfers between devices: 17 us -> 12.4 us  [body(): lax.all_to_all(spread, axes, 0, 0, tiled=False)]
    ppermute x1, starting transfers between devices: 5.1 us -> 1.92 us  [with_halo(): lax.ppermute(lax.slice_in_dim(block, 0, width, axis=dim), axis, backward)]
    ppermute x1, starting transfers between devices: 3.02 us -> 6.2 us  [with_halo(): lax.ppermute(lax.slice_in_dim(block, block.shape[dim] - width, None, axis...]
    concatenate x1 -> x0, other arithmetic: 2.14 us -> none  [body(): everything = jnp.concatenate([everything, partner], axis=0)]
    dot_general x0 -> x1, matrix products: none -> 1.3 us  [body(): jnp.einsum('lkq,lrq->lrk', leaf_coupling, side_by_side(far_skels), prefer...]
    dot_general x1, matrix products: 1.24 us -> 0.29 us  [body(): jnp.einsum('crk,ckq->crq', coarse_field, transfer, preferred_element_type...]
  transfers between devices with their start and end apart: 5 -> 5, of which waited for: 2 -> 3; matrix products, arithmetic and copies ran while one was open for 12% -> 26% of each run, Pallas kernels for 0% -> 0%
where the time goes in v5:
time: 53.5 us; the launch traced here: 53.1 us
  starting transfers between devices  26.8 us (50%)
  matrix products  9.74 us (18%)
  local copies, waits for them, and re-layouts  8.77 us (16%)
  waiting for transfers between devices  6.5 us (12%)
  other arithmetic  1.03 us (2%)
    all_to_all x2, starting transfers between devices, body(): lax.all_to_all(spread, axes, 0, 0, tiled=False)  12.4 us
    ppermute x1, starting transfers between devices, body(): partner = lax.ppermute(everything, PAIR, [(0, 1), (1, 0)])  6.21 us
    ppermute x1, starting transfers between devices, with_halo(): lax.ppermute(lax.slice_in_dim(block, block.shape[dim] - width, None, axis...  6.2 us
    all_to_all x2, waiting for transfers between devices, body(): lax.all_to_all(spread, axes, 0, 0, tiled=False)  5.61 us
    dot_general x1, matrix products, body(): jnp.einsum('ljpq,ljrq->lrp', near_blocks, near_rows, preferred_element_ty...  4.6 us
    ppermute x1, starting transfers between devices, with_halo(): lax.ppermute(lax.slice_in_dim(block, 0, width, axis=dim), axis, backward)  1.92 us
    gather x1, local copies, waits for them, and re-layouts, body(): jnp.take(partner, row, axis=0)  1.74 us
    broadcast_in_dim x4, local copies, waits for them, and re-layouts, body(): spread = jnp.broadcast_to(everything[None], (n,) + everything.shape)  1.6 us
  transfers between devices with their start and end apart: 5, of which 3 were waited for; matrix products, arithmetic and copies ran while one was open for 26% of the time, Pallas kernels for 0%

profile of v5, /device:TPU:1, one launch (start us, length us, event | category | flops | bytes accessed | tf_op | source)
XLA Modules:
  0.0 53.1 jit_solution(15034446329958201156)
XLA Ops:
  0.0 1.6 %convolution_convert_fusion = bf16[32,8,64]{2,1,0:T(8,128)(2,1)S(1)} fusion(bf16[32,8,128]{2,1,0:T(8,128)(2,1)} %param.11, bf16[32,64,128]{2,1,0:T(8,128)(2,1)} %param.12), kind=kOutput, calls=%fused_computation.7 | convolution fusion | flops 4210688 | bytes 622592 | tf_op jit(solution)/shard_map/lrp,lkp->lrk/dot_general | solution.py:46
  1.6 0.1 reshape.56
  1.7 0.9 %bitcast_dynamic-update-slice_fusion = bf16[32,1536]{1,0:T(8,128)(2,1)S(1)} fusion(bf16[4,8,8,128]{3,2,1,0:T(8,128)(2,1)} %bitcast.51), kind=kLoop, calls=%fused_computation.20 | loop fusion | bytes 131072
  2.6 6.2 %collective-permute-start = (bf16[32,1536]{1,0:T(8,128)(2,1)S(1)}, bf16[32,1536]{1,0:T(8,128)(2,1)S(1)}, u32[]{:S(2)}, u32[]{:S(2)}) collective-permute-start(bf16[32,1536]{1,0:T(8,128)(2,1)S(1)} %constant_dynamic-update-slice_fusion), channel_id=1, source_target_pairs={{0,1},{1,2},{2,3},{3,4},{4,5},{5,6},{6,7},{7,8},{8,9},{9,10},{10,1... | collective-permute-start | bytes 294920 | tf_op jit(solution)/shard_map/ppermute | solution.py:16
  8.8 1.9 %collective-permute-start.1 = (bf16[32,1536]{1,0:T(8,128)(2,1)S(1)}, bf16[32,1536]{1,0:T(8,128)(2,1)S(1)}, u32[]{:S(2)}, u32[]{:S(2)}) collective-permute-start(bf16[32,1536]{1,0:T(8,128)(2,1)S(1)} %constant_dynamic-update-slice_fusion), channel_id=1, source_target_pairs={{1,0},{2,1},{3,2},{4,3},{5,4},{6,5},{7,6},{8,7},{9,8},{10,9},{11,1... | collective-permute-start | bytes 294920 | tf_op jit(solution)/shard_map/ppermute | solution.py:19
  10.8 1.1 %convolution_convert_fusion.2 = bf16[4,8,64]{2,1,0:T(8,128)(2,1)S(1)} fusion(bf16[4,8,512]{2,1,0:T(8,128)(2,1)S(1)} %reshape.53, bf16[4,64,512]{2,1,0:T(8,128)(2,1)} %param.17), kind=kOutput, calls=%fused_computation.9 | convolution fusion | flops 2099200 | bytes 299008 | tf_op jit(solution)/shard_map/ckq,crq->crk/dot_general | solution.py:50
  12.0 0.6 %broadcast_in_dim.57 = bf16[8,4,512]{2,1,0:T(4,128)(2,1)} broadcast(bf16[4,512]{1,0:T(4,128)(2,1)S(1)} %broadcast_in_dim.56), dimensions={1,2} | broadcast | bytes 36864 | tf_op jit(solution)/shard_map/broadcast_in_dim | solution.py:57
  12.7 8.2 %all-to-all-start = ((bf16[8,4,512]{2,1,0:T(4,128)(2,1)}), bf16[8,4,512]{2,1,0:T(4,128)(2,1)S(1)}, u32[]{:S(2)}, u32[]{:S(2)}) async-start(bf16[8,4,512]{2,1,0:T(4,128)(2,1)} %broadcast_in_dim.57), calls=%async_computation | async-start | bytes 65536 | tf_op jit(solution)/shard_map/all_to_all | solution.py:58
  20.9 0.7 %compare_and_fusion = (pred[32,6]{0,1:T(8,128)(4,1)S(1)}, s32[32,6]{0,1:T(8,128)S(1)}, pred[32,6]{0,1:T(8,128)(4,1)S(1)}, s32[32,6]{0,1:T(8,128)S(1)}) fusion(s32[32,6]{0,1:T(8,128)} %param.15, s32[]{:T(128)S(6)} %sub.35, s32[32,6]{0,1:T(8,128)} %param.13), kind=kLoop, calls=%fused_computation.31 | loop fusion | flops 2688 | bytes 3460 | tf_op jit(solution)/shard_map/jit(_take)/and | solution.py:75
  22.2 5.6 %all-to-all-done = bf16[8,4,512]{2,1,0:T(4,128)(2,1)S(1)} async-done(((bf16[8,4,512]{2,1,0:T(4,128)(2,1)}), bf16[8,4,512]{2,1,0:T(4,128)(2,1)S(1)}, u32[]{:S(2)}, u32[]{:S(2)}) %all-to-all-start) | async-done | bytes 32800 | tf_op jit(solution)/shard_map/all_to_all | solution.py:58
  27.8 0.8 %broadcast_in_dim.59 = bf16[16,32,512]{2,1,0:T(8,128)(2,1)} broadcast(bf16[32,512]{1,0:T(8,128)(2,1)S(1)} %broadcast_in_dim.58), dimensions={1,2} | broadcast | bytes 557056 | tf_op jit(solution)/shard_map/broadcast_in_dim | solution.py:57
  28.6 4.2 %all-to-all-start.1 = ((bf16[16,32,512]{2,1,0:T(8,128)(2,1)}), bf16[16,32,512]{2,1,0:T(8,128)(2,1)S(1)}, u32[]{:S(2)}, u32[]{:S(2)}) async-start(bf16[16,32,512]{2,1,0:T(8,128)(2,1)} %broadcast_in_dim.59), calls=%async_computation.1 | async-start | bytes 1048576 | tf_op jit(solution)/shard_map/all_to_all | solution.py:58
  32.9 1.0 %gather_fusion.1 = bf16[192,512]{1,0:T(8,128)(2,1)S(1)} fusion(bf16[96,512]{1,0:T(8,128)(2,1)S(1)} %pad_maximum_fusion.1, s32[1024]{0:T(1024)S(1)} %pad_clamp_fusion.1), kind=kCustom, calls=%fused_computation.3 | custom fusion | bytes 393984 | tf_op jit(solution)/shard_map/jit(_take)/gather | solution.py:75
  33.9 0.2 gather.18
  34.3 0.3 reshape.57
  34.6 1.3 %fusion.25 = f32[32,8,64]{2,1,0:T(8,128)} fusion(bf16[32,8,384]{2,1,0:T(8,128)(2,1)S(1)} %reshape.57, bf16[32,64,384]{2,1,0:T(8,128)(2,1)S(1)} %copy-done), kind=kOutput, calls=%fused_computation.86 | convolution fusion | flops 12582912 | bytes 1835008 | tf_op jit(solution)/shard_map/lkq,lrq->lrk/dot_general | solution.py:78
  36.0 1.0 %gather_fusion = bf16[192,1024]{1,0:T(8,128)(2,1)S(1)} fusion(bf16[96,1024]{1,0:T(8,128)(2,1)S(1)} %slice.16, s32[1024]{0:T(1024)S(1)} %pad_clamp_fusion.2), kind=kCustom, calls=%fused_computation.2 | custom fusion | bytes 787200 | tf_op jit(solution)/shard_map/jit(_take)/gather | solution.py:69
  37.1 4.6 %convolution_bitcast_fusion = f32[32,8,128]{2,1,0:T(8,128)S(1)} fusion(bf16[32,6,128,128]{3,2,1,0:T(8,128)(2,1)} %param.14, bf16[32,6,8,128]{3,2,1,0:T(8,128)(2,1)S(1)} %bitcast.47, pred[32,6]{1,0:T(8,128)(4,1)S(1)} %copy.23), kind=kOutput, calls=%fused_computation.5 | convolution fusion | flops 50528256 | bytes 6815936 | tf_op jit(solution)/shard_map/ljpq,ljrq->lrp/dot_general | solution.py:72
  41.7 6.2 %collective-permute-start.2 = (bf16[512,512]{1,0:T(8,128)(2,1)S(1)}, bf16[512,512]{1,0:T(8,128)(2,1)}, u32[]{:S(2)}, u32[]{:S(2)}) collective-permute-start(bf16[512,512]{1,0:T(8,128)(2,1)S(1)} %bitcast.48), channel_id=1, source_target_pairs={{0,1},{1,0},{2,3},{3,2},{4,5},{5,4},{6,7},{7,6},{8,9},{9,8},{10,11... | collective-permute-start | bytes 1572872 | tf_op jit(solution)/shard_map/ppermute | solution.py:82
  48.1 0.6 %gather_fusion.3 = bf16[32,512]{1,0:T(8,128)(2,1)S(1)} fusion(bf16[512,512]{1,0:T(8,128)(2,1)S(1)} %bitcast.49, s32[1024]{0:T(1024)S(1)} %pad_clamp_fusion), kind=kCustom, calls=%fused_computation.1.clone | custom fusion | bytes 65664 | tf_op jit(solution)/shard_map/jit(_take)/gather | solution.py:98
  48.7 0.9 %collective-permute-done.2 = bf16[512,512]{1,0:T(8,128)(2,1)} collective-permute-done((bf16[512,512]{1,0:T(8,128)(2,1)S(1)}, bf16[512,512]{1,0:T(8,128)(2,1)}, u32[]{:S(2)}, u32[]{:S(2)}) %collective-permute-start.2) | collective-permute-done | bytes 524320 | tf_op jit(solution)/shard_map/ppermute | solution.py:82
  49.6 1.7 %gather_fusion.2 = bf16[32,512]{1,0:T(8,128)(2,1)S(1)} fusion(bf16[512,512]{1,0:T(8,128)(2,1)} %collective-permute-done.2, s32[1024]{0:T(1024)S(1)} %pad_clamp_fusion), kind=kCustom, calls=%fused_computation.clone | custom fusion | bytes 65664 | tf_op jit(solution)/shard_map/jit(_take)/gather | solution.py:97
  51.7 0.3 fusion.1
  52.2 0.9 %fusion = bf16[32,8,128]{2,1,0:T(8,128)(2,1)} fusion(f32[32,8,128]{2,1,0:T(8,128)S(1)} %convolution_bitcast_fusion, bf16[32,8,64]{2,1,0:T(8,128)(2,1)S(1)} %fusion.6, bf16[32,64,128]{2,1,0:T(8,128)(2,1)S(1)} %copy-done.1), kind=kOutput, calls=%fused_computation.6 | convolution fusion | flops 4259840 | bytes 753664 | tf_op jit(solution)/shard_map/lrk,lkp->lrp/dot_general | solution.py:113
  (43 shorter events, 1.8 us)
Async XLA Ops:
  0.0 34.6 %copy-start = (bf16[32,64,384]{2,1,0:T(8,128)(2,1)S(1)}, bf16[32,64,384]{2,1,0:T(8,128)(2,1)}, u32[]{:S(2)}) copy-start(bf16[32,64,384]{2,1,0:T(8,128)(2,1)} %param.16) | copy-start | bytes 4718596
  2.6 30.3 %collective-permute-start = (bf16[32,1536]{1,0:T(8,128)(2,1)S(1)}, bf16[32,1536]{1,0:T(8,128)(2,1)S(1)}, u32[]{:S(2)}, u32[]{:S(2)}) collective-permute-start(bf16[32,1536]{1,0:T(8,128)(2,1)S(1)} %constant_dynamic-update-slice_fusion), channel_id=1, source_target_pairs={{0,1},{1,2},{2,3},{3,4},{4,5},{5,6},{6,7},{7,8},{8,9},{9,10},{10,1... | collective-permute-start | bytes 294920 | tf_op jit(solution)/shard_map/ppermute | solution.py:16
  8.8 24.1 %collective-permute-start.1 = (bf16[32,1536]{1,0:T(8,128)(2,1)S(1)}, bf16[32,1536]{1,0:T(8,128)(2,1)S(1)}, u32[]{:S(2)}, u32[]{:S(2)}) collective-permute-start(bf16[32,1536]{1,0:T(8,128)(2,1)S(1)} %constant_dynamic-update-slice_fusion), channel_id=1, source_target_pairs={{1,0},{2,1},{3,2},{4,3},{5,4},{6,5},{7,6},{8,7},{9,8},{10,9},{11,1... | collective-permute-start | bytes 294920 | tf_op jit(solution)/shard_map/ppermute | solution.py:19
  12.7 15.1 %all-to-all-start = ((bf16[8,4,512]{2,1,0:T(4,128)(2,1)}), bf16[8,4,512]{2,1,0:T(4,128)(2,1)S(1)}, u32[]{:S(2)}, u32[]{:S(2)}) async-start(bf16[8,4,512]{2,1,0:T(4,128)(2,1)} %broadcast_in_dim.57), calls=%async_computation | async-start | bytes 65536 | tf_op jit(solution)/shard_map/all_to_all | solution.py:58
  28.6 13.1 %all-to-all-start.1 = ((bf16[16,32,512]{2,1,0:T(8,128)(2,1)}), bf16[16,32,512]{2,1,0:T(8,128)(2,1)S(1)}, u32[]{:S(2)}, u32[]{:S(2)}) async-start(bf16[16,32,512]{2,1,0:T(8,128)(2,1)} %broadcast_in_dim.59), calls=%async_computation.1 | async-start | bytes 1048576 | tf_op jit(solution)/shard_map/all_to_all | solution.py:58
  35.9 12.0 %copy-start.5 = (s32[4,8]{1,0:T(4,128)S(1)}, s32[4,8]{1,0:T(4,128)}, u32[]{:S(2)}) copy-start(s32[4,8]{1,0:T(4,128)} %param.18) | copy-start | bytes 388
  36.0 15.7 %copy-start.2 = (bf16[4,64,512]{2,1,0:T(8,128)(2,1)S(1)}, bf16[4,64,512]{2,1,0:T(8,128)(2,1)}, u32[]{:S(2)}) copy-start(bf16[4,64,512]{2,1,0:T(8,128)(2,1)} %param.17) | copy-start | bytes 786436
  36.0 16.2 %copy-start.1 = (bf16[32,64,128]{2,1,0:T(8,128)(2,1)S(1)}, bf16[32,64,128]{2,1,0:T(8,128)(2,1)}, u32[]{:S(2)}) copy-start(bf16[32,64,128]{2,1,0:T(8,128)(2,1)} %param.12) | copy-start | bytes 1572868
  37.1 14.6 %copy-start.4 = (bf16[4,64,512]{2,1,0:T(8,128)(2,1)S(1)}, bf16[4,64,512]{2,1,0:T(8,128)(2,1)}, u32[]{:S(2)}) copy-start(bf16[4,64,512]{2,1,0:T(8,128)(2,1)} %param.19) | copy-start | bytes 786436
  37.1 15.1 %copy-start.3 = (f32[32,8,64]{2,1,0:T(8,128)S(1)}, f32[32,8,64]{2,1,0:T(8,128)}, u32[]{:S(2)}) copy-start(f32[32,8,64]{2,1,0:T(8,128)} %fusion.25) | copy-start | bytes 196612
  41.7 7.9 %collective-permute-start.2 = (bf16[512,512]{1,0:T(8,128)(2,1)S(1)}, bf16[512,512]{1,0:T(8,128)(2,1)}, u32[]{:S(2)}, u32[]{:S(2)}) collective-permute-start(bf16[512,512]{1,0:T(8,128)(2,1)S(1)} %bitcast.48), channel_id=1, source_target_pairs={{0,1},{1,0},{2,3},{3,2},{4,5},{5,4},{6,7},{7,6},{8,9},{9,8},{10,11... | collective-permute-start | bytes 1572872 | tf_op jit(solution)/shard_map/ppermute | solution.py:82

commit v6 on v3

--- a/solution.py
+++ b/solution.py
@@ -6,19 +6,6 @@
 ALL = ("z", "x", "y_lo", "y_hi", "core")
 STAGES = (("z",), ("x", "y_lo", "y_hi"))
 PAIR = "core"
-
-
-def with_halo(block, sides, width):
-    for axis, dim in sides:
-        count = lax.axis_size(axis)
-        forward = [(i, i + 1) for i in range(count - 1)]
-        backward = [(target, source) for source, target in forward]
-        low = lax.ppermute(
-            lax.slice_in_dim(block, block.shape[dim] - width, None, axis=dim), axis, forward
-        )
-        high = lax.ppermute(lax.slice_in_dim(block, 0, width, axis=dim), axis, backward)
-        block = jnp.concatenate([low, block, high], axis=dim)
-    return block
 
 
 def side_by_side(parts):
@@ -51,35 +38,53 @@
         "ckq,crq->crk", transfer, side_by_side(children), preferred_element_type=jnp.float32
     ).astype(jnp.bfloat16)
     coarse_flat = coarse.reshape(box_count, rhs_count * rank_width)
-    everything = coarse_flat
+    density_flat = density.reshape(leaf_count, rhs_count * leaf_width)
+    skeleton_flat = skeleton.reshape(leaf_count, rhs_count * rank_width)
+    device_count = lax.axis_size(ALL)
+    me = lax.axis_index(ALL)
+    even = lax.axis_index(PAIR) == 0
+    own = jnp.concatenate([density_flat, skeleton_flat], axis=1)
+    cross_pairs = [(d, d + 1) for d in range(1, device_count - 1, 2)]
+    cross_pairs += [(d + 1, d) for d in range(1, device_count - 1, 2)]
+    cross = lax.ppermute(own, ALL, cross_pairs)
+    width = own.shape[1]
+    coarse_rows = -(-coarse_flat.size // width)
+    packed = jnp.pad(coarse_flat.reshape(1, -1), ((0, 0), (0, coarse_rows * width - coarse_flat.size)))
+    received = lax.ppermute(
+        jnp.concatenate([own, packed.reshape(coarse_rows, width)], axis=0), PAIR, [(0, 1), (1, 0)]
+    )
+    pair_halo = received[:leaf_count]
+    pair_coarse = received[leaf_count:].reshape(-1)[: coarse_flat.size].reshape(coarse_flat.shape)
+    padded = jnp.concatenate([pair_halo, own, cross], axis=0)
+    density_padded = padded[:, : density_flat.shape[1]]
+    skeleton_padded = padded[:, density_flat.shape[1] :]
+    everything = jnp.concatenate([coarse_flat, pair_coarse], axis=0)
     for axes in STAGES:
         n = lax.axis_size(axes)
         spread = jnp.broadcast_to(everything[None], (n,) + everything.shape)
         everything = lax.all_to_all(spread, axes, 0, 0, tiled=False).reshape(
             (n * everything.shape[0],) + everything.shape[1:]
         )
-    partner = lax.ppermute(everything, PAIR, [(0, 1), (1, 0)])
-    everything = jnp.concatenate([everything, partner], axis=0)
-    offset_base = lax.axis_index(ALL) * leaf_count - leaf_count
-    density_flat = density.reshape(leaf_count, rhs_count * leaf_width)
-    skeleton_flat = skeleton.reshape(leaf_count, rhs_count * rank_width)
-    both_padded = with_halo(
-        jnp.concatenate([density_flat, skeleton_flat], axis=1), ((ALL, 0),), leaf_count
-    )
-    density_padded = both_padded[:, : density_flat.shape[1]]
-    skeleton_padded = both_padded[:, density_flat.shape[1] :]
-    near_rows = jnp.take(density_padded, near_list - offset_base, axis=0).reshape(
+
+    def halo_row(index):
+        t = index - me * leaf_count
+        low = jnp.where(even, t + 3 * leaf_count, t + leaf_count)
+        high = jnp.where(even, t - leaf_count, t + leaf_count)
+        return jnp.where(t < 0, low, jnp.where(t < leaf_count, t + leaf_count, high))
+    near_rows = jnp.take(density_padded, halo_row(near_list), axis=0).reshape(
         leaf_count, near_list.shape[1], rhs_count, leaf_width
     )
     near_part = jnp.einsum(
         "ljpq,ljrq->lrp", near_blocks, near_rows, preferred_element_type=jnp.float32
     )
-    far_skels = jnp.take(skeleton_padded, far_leaf - offset_base, axis=0).reshape(
+    far_skels = jnp.take(skeleton_padded, halo_row(far_leaf), axis=0).reshape(
         leaf_count, far_count, rhs_count, rank_width
     )
     leaf_far = jnp.einsum(
         "lkq,lrq->lrk", leaf_coupling, side_by_side(far_skels), preferred_element_type=jnp.float32
     )
+    everything, near_part, leaf_far = lax.optimization_barrier((everything, near_part, leaf_far))
+
     sizes = [lax.axis_size(a) for a in ALL]
     owner, slot = far_coarse // box_count, far_coarse % box_count
     coords = []
@@ -87,10 +92,11 @@
         coords.append(owner % size)
         owner = owner // size
     coords = dict(zip(reversed(ALL), coords))
-    position = (coords[PAIR] != lax.axis_index(PAIR)).astype(jnp.int32)
+    position = 0
     for axes in reversed(STAGES):
         for a in axes:
             position = position * lax.axis_size(a) + coords[a]
+    position = position * 2 + (coords[PAIR] != lax.axis_index(PAIR)).astype(jnp.int32)
     coarse_skels = jnp.take(everything, position * box_count + slot, axis=0).reshape(
         box_count, coarse_count, rhs_count, rank_width
     )

time: 64.6 us -> 58.8 us (0.910)
  the two profiles are of different devices: /device:TPU:1 before, /device:TPU:8 now
where the time goes in v6:
time: 58.8 us; the launch traced here: 58.3 us
  starting transfers between devices  19.7 us (34%)
  waiting for transfers between devices  17.8 us (30%)
  matrix products  10.1 us (17%)
  local copies, waits for them, and re-layouts  8.81 us (15%)
  other arithmetic  1.74 us (3%)
    all_to_all x2, waiting for transfers between devices, body(): lax.all_to_all(spread, axes, 0, 0, tiled=False)  17.8 us
    all_to_all x2, starting transfers between devices, body(): lax.all_to_all(spread, axes, 0, 0, tiled=False)  15.3 us
    dot_general x1, matrix products, body(): jnp.einsum('ljpq,ljrq->lrp', near_blocks, near_rows, preferred_element_ty...  4.56 us
    ppermute x1, starting transfers between devices, body(): cross = lax.ppermute(own, ALL, cross_pairs)  2.92 us
    gather x2, local copies, waits for them, and re-layouts, body(): jnp.take(everything, position * box_count + slot, axis=0)  2.09 us
    broadcast_in_dim x2, local copies, waits for them, and re-layouts, body(): spread = jnp.broadcast_to(everything[None], (n,) + everything.shape)  1.77 us
    dot_general x1, matrix products, body(): jnp.einsum('lrp,lkp->lrk', density, basis, preferred_element_type=jnp.flo...  1.56 us
    ppermute x1, starting transfers between devices, body(): lax.ppermute(jnp.concatenate([own, packed.reshape(coarse_rows, width)], a...  1.48 us
  transfers between devices with their start and end apart: 4, of which 2 were waited for; matrix products, arithmetic and copies ran while one was open for 21% of the time, Pallas kernels for 0%

profile of v6, /device:TPU:8, one launch (start us, length us, event | category | flops | bytes accessed | tf_op | source)
XLA Modules:
  0.0 58.3 jit_solution(838947466469946428)
XLA Ops:
  0.0 1.6 %convolution_convert_fusion = bf16[32,8,64]{2,1,0:T(8,128)(2,1)S(1)} fusion(bf16[32,8,128]{2,1,0:T(8,128)(2,1)} %param.9, bf16[32,64,128]{2,1,0:T(8,128)(2,1)} %param.10), kind=kOutput, calls=%fused_computation.6 | convolution fusion | flops 4210688 | bytes 622592 | tf_op jit(solution)/shard_map/lrp,lkp->lrk/dot_general | solution.py:33
  1.6 0.9 %bitcast_dynamic-update-slice_fusion = bf16[32,1536]{1,0:T(8,128)(2,1)S(1)} fusion(bf16[4,8,8,128]{3,2,1,0:T(8,128)(2,1)} %bitcast.43), kind=kLoop, calls=%fused_computation.20 | loop fusion | bytes 131072
  2.6 2.9 %collective-permute-start.1 = (bf16[32,1536]{1,0:T(8,128)(2,1)S(1)}, bf16[32,1536]{1,0:T(8,128)(2,1)S(1)}, u32[]{:S(2)}, u32[]{:S(2)}) collective-permute-start(bf16[32,1536]{1,0:T(8,128)(2,1)S(1)} %constant_dynamic-update-slice_fusion), channel_id=1, source_target_pairs={{1,2},{3,4},{5,6},{7,8},{9,10},{11,12},{13,14},{15,16},{17,18},{19... | collective-permute-start | bytes 294920 | tf_op jit(solution)/shard_map/ppermute | solution.py:49
  5.5 0.1 reshape.61
  5.6 1.1 %convolution_convert_fusion.2 = bf16[4,8,64]{2,1,0:T(8,128)(2,1)S(1)} fusion(bf16[4,8,512]{2,1,0:T(8,128)(2,1)S(1)} %reshape.61, bf16[4,64,512]{2,1,0:T(8,128)(2,1)} %param.15), kind=kOutput, calls=%fused_computation.8 | convolution fusion | flops 2099200 | bytes 299008 | tf_op jit(solution)/shard_map/ckq,crq->crk/dot_general | solution.py:37
  6.9 1.5 %collective-permute-start = (bf16[34,1536]{1,0:T(8,128)(2,1)S(1)}, bf16[34,1536]{1,0:T(8,128)(2,1)S(1)}, u32[]{:S(2)}, u32[]{:S(2)}) collective-permute-start(bf16[34,1536]{1,0:T(8,128)(2,1)S(1)} %pad_maximum_fusion.1), channel_id=1, source_target_pairs={{0,1},{1,0},{2,3},{3,2},{4,5},{5,4},{6,7},{7,6},{8,9},{9,8},{10,11... | collective-permute-start | bytes 313352 | tf_op jit(solution)/shard_map/ppermute | solution.py:53
  8.5 0.7 %compare_and_fusion = (pred[32,6]{0,1:T(8,128)(4,1)S(1)}, s32[32,6]{0,1:T(8,128)S(1)}, pred[32,6]{0,1:T(8,128)(4,1)S(1)}, s32[32,6]{0,1:T(8,128)S(1)}) fusion(pred[]{:T(512)S(6)} %eq.10, s32[32,6]{0,1:T(8,128)} %param.13, s32[]{:T(128)S(6)} %mul.39, s32[32,6]{0,1:T(8,128)} %param.11), kind=kLoop, calls=%fused_computation.36 | loop fusion | flops 6144 | bytes 3461 | tf_op jit(solution)/shard_map/jit(_take)/and | solution.py:80
  9.8 0.7 %compare_and_fusion.2 = (pred[4,8]{1,0:T(4,128)(4,1)S(1)}, s32[4,8]{1,0:T(4,128)S(1)}) fusion(s32[]{:T(128)S(6)} %axis_index.60, s32[4,8]{1,0:T(4,128)} %param.16), kind=kLoop, calls=%fused_computation.87 | loop fusion | flops 3968 | bytes 292 | tf_op jit(solution)/shard_map/jit(_take)/and | solution.py:100
  10.7 0.6 %broadcast_in_dim.49 = bf16[8,8,512]{2,1,0:T(8,128)(2,1)} broadcast(bf16[8,512]{1,0:T(8,128)(2,1)S(1)} %pad_maximum_fusion.3), dimensions={1,2} | broadcast | bytes 73728 | tf_op jit(solution)/shard_map/broadcast_in_dim | solution.py:64
  11.4 8.5 %all-to-all-start = ((bf16[8,8,512]{2,1,0:T(8,128)(2,1)}), bf16[8,8,512]{2,1,0:T(8,128)(2,1)S(1)}, u32[]{:S(2)}, u32[]{:S(2)}) async-start(bf16[8,8,512]{2,1,0:T(8,128)(2,1)} %broadcast_in_dim.49), calls=%async_computation | async-start | bytes 131072 | tf_op jit(solution)/shard_map/all_to_all | solution.py:65
  19.9 8.3 %all-to-all-done = bf16[8,8,512]{2,1,0:T(8,128)(2,1)S(1)} async-done(((bf16[8,8,512]{2,1,0:T(8,128)(2,1)}), bf16[8,8,512]{2,1,0:T(8,128)(2,1)S(1)}, u32[]{:S(2)}, u32[]{:S(2)}) %all-to-all-start) | async-done | bytes 65568 | tf_op jit(solution)/shard_map/all_to_all | solution.py:65
  28.2 1.1 %broadcast_in_dim.51 = bf16[16,64,512]{2,1,0:T(8,128)(2,1)} broadcast(bf16[64,512]{1,0:T(8,128)(2,1)S(1)} %bitcast.44), dimensions={1,2} | broadcast | bytes 1114112 | tf_op jit(solution)/shard_map/broadcast_in_dim | solution.py:64
  29.3 6.8 %all-to-all-start.1 = ((bf16[16,64,512]{2,1,0:T(8,128)(2,1)}), bf16[16,64,512]{2,1,0:T(8,128)(2,1)}, u32[]{:S(2)}, u32[]{:S(2)}) async-start(bf16[16,64,512]{2,1,0:T(8,128)(2,1)} %broadcast_in_dim.51), calls=%async_computation.1 | async-start | bytes 2097152 | tf_op jit(solution)/shard_map/all_to_all | solution.py:65
  36.2 1.0 %gather_fusion = bf16[192,1024]{1,0:T(8,128)(2,1)S(1)} fusion(bf16[96,1024]{1,0:T(8,128)(2,1)S(1)} %slice.33, s32[1024]{0:T(1024)S(1)} %pad_clamp_fusion.2), kind=kCustom, calls=%fused_computation | custom fusion | bytes 787200 | tf_op jit(solution)/shard_map/jit(_take)/gather | solution.py:74
  37.3 1.0 %gather_fusion.1 = bf16[192,512]{1,0:T(8,128)(2,1)S(1)} fusion(bf16[96,512]{1,0:T(8,128)(2,1)S(1)} %pad_maximum_fusion.2, s32[1024]{0:T(1024)S(1)} %pad_clamp_fusion.1), kind=kCustom, calls=%fused_computation.1 | custom fusion | bytes 393984 | tf_op jit(solution)/shard_map/jit(_take)/gather | solution.py:80
  38.3 0.2 gather.21
  38.6 0.3 reshape.67
  39.0 0.6 %fusion.28 = f32[32,8,64]{2,1,0:T(8,128)S(1)} fusion(bf16[32,8,384]{2,1,0:T(8,128)(2,1)S(1)} %reshape.67, bf16[32,64,384]{2,1,0:T(8,128)(2,1)S(1)} %copy-done), kind=kOutput, calls=%fused_computation.90 | convolution fusion | flops 12582912 | bytes 1835008 | tf_op jit(solution)/shard_map/lkq,lrq->lrk/dot_general | solution.py:83
  39.6 4.6 %convolution_bitcast_fusion = f32[32,8,128]{2,1,0:T(8,128)S(1)} fusion(bf16[32,6,128,128]{3,2,1,0:T(8,128)(2,1)} %param.12, bf16[32,6,8,128]{3,2,1,0:T(8,128)(2,1)S(1)} %bitcast.41, pred[32,6]{1,0:T(8,128)(4,1)S(1)} %copy.16), kind=kOutput, calls=%fused_computation.4 | convolution fusion | flops 50528256 | bytes 6815936 | tf_op jit(solution)/shard_map/ljpq,ljrq->lrp/dot_general | solution.py:77
  44.2 9.4 %all-to-all-done.1 = bf16[16,64,512]{2,1,0:T(8,128)(2,1)} async-done(((bf16[16,64,512]{2,1,0:T(8,128)(2,1)}), bf16[16,64,512]{2,1,0:T(8,128)(2,1)}, u32[]{:S(2)}, u32[]{:S(2)}) %all-to-all-start.1) | async-done | bytes 1048608 | tf_op jit(solution)/shard_map/all_to_all | solution.py:65
  53.6 2.0 %gather_fusion.2 = bf16[32,512]{1,0:T(8,128)(2,1)S(1)} fusion(bf16[1024,512]{1,0:T(8,128)(2,1)} %bitcast.3, s32[1024]{0:T(1024)S(1)} %pad_clamp_fusion), kind=kCustom, calls=%fused_computation.2 | custom fusion | bytes 65664 | tf_op jit(solution)/shard_map/jit(_take)/gather | solution.py:100
  55.8 0.1 reshape.68
  55.9 1.3 %fusion.1 = f32[4,8,512]{2,1,0:T(8,128)S(1)} fusion(bf16[4,64,512]{2,1,0:T(8,128)(2,1)} %param.15, bf16[4,8,512]{2,1,0:T(8,128)(2,1)S(1)} %reshape.68, bf16[4,64,512]{2,1,0:T(8,128)(2,1)} %param.17), kind=kOutput, calls=%fused_computation.9 | convolution fusion | flops 4196352 | bytes 622592 | tf_op jit(solution)/shard_map/crk,ckq->crq/dot_general | solution.py:106
  57.4 0.9 %fusion = bf16[32,8,128]{2,1,0:T(8,128)(2,1)} fusion(f32[32,8,128]{2,1,0:T(8,128)S(1)} %convolution_bitcast_fusion, bf16[32,8,64]{2,1,0:T(8,128)(2,1)S(1)} %fusion.6, bf16[32,64,128]{2,1,0:T(8,128)(2,1)S(1)} %copy-done.1), kind=kOutput, calls=%fused_computation.5 | convolution fusion | flops 4259840 | bytes 753664 | tf_op jit(solution)/shard_map/lrk,lkp->lrp/dot_general | solution.py:116
  (39 shorter events, 1.7 us)
Async XLA Ops:
  0.0 39.0 %copy-start = (bf16[32,64,384]{2,1,0:T(8,128)(2,1)S(1)}, bf16[32,64,384]{2,1,0:T(8,128)(2,1)}, u32[]{:S(2)}) copy-start(bf16[32,64,384]{2,1,0:T(8,128)(2,1)} %param.14) | copy-start | bytes 4718596
  2.6 17.3 %collective-permute-start.1 = (bf16[32,1536]{1,0:T(8,128)(2,1)S(1)}, bf16[32,1536]{1,0:T(8,128)(2,1)S(1)}, u32[]{:S(2)}, u32[]{:S(2)}) collective-permute-start(bf16[32,1536]{1,0:T(8,128)(2,1)S(1)} %constant_dynamic-update-slice_fusion), channel_id=1, source_target_pairs={{1,2},{3,4},{5,6},{7,8},{9,10},{11,12},{13,14},{15,16},{17,18},{19... | collective-permute-start | bytes 294920 | tf_op jit(solution)/shard_map/ppermute | solution.py:49
  6.9 3.7 %collective-permute-start = (bf16[34,1536]{1,0:T(8,128)(2,1)S(1)}, bf16[34,1536]{1,0:T(8,128)(2,1)S(1)}, u32[]{:S(2)}, u32[]{:S(2)}) collective-permute-start(bf16[34,1536]{1,0:T(8,128)(2,1)S(1)} %pad_maximum_fusion.1), channel_id=1, source_target_pairs={{0,1},{1,0},{2,3},{3,2},{4,5},{5,4},{6,7},{7,6},{8,9},{9,8},{10,11... | collective-permute-start | bytes 313352 | tf_op jit(solution)/shard_map/ppermute | solution.py:53
  11.4 16.8 %all-to-all-start = ((bf16[8,8,512]{2,1,0:T(8,128)(2,1)}), bf16[8,8,512]{2,1,0:T(8,128)(2,1)S(1)}, u32[]{:S(2)}, u32[]{:S(2)}) async-start(bf16[8,8,512]{2,1,0:T(8,128)(2,1)} %broadcast_in_dim.49), calls=%async_computation | async-start | bytes 131072 | tf_op jit(solution)/shard_map/all_to_all | solution.py:65
  29.3 24.2 %all-to-all-start.1 = ((bf16[16,64,512]{2,1,0:T(8,128)(2,1)}), bf16[16,64,512]{2,1,0:T(8,128)(2,1)}, u32[]{:S(2)}, u32[]{:S(2)}) async-start(bf16[16,64,512]{2,1,0:T(8,128)(2,1)} %broadcast_in_dim.51), calls=%async_computation.1 | async-start | bytes 2097152 | tf_op jit(solution)/shard_map/all_to_all | solution.py:65
  38.5 18.9 %copy-start.1 = (bf16[32,64,128]{2,1,0:T(8,128)(2,1)S(1)}, bf16[32,64,128]{2,1,0:T(8,128)(2,1)}, u32[]{:S(2)}) copy-start(bf16[32,64,128]{2,1,0:T(8,128)(2,1)} %param.10) | copy-start | bytes 1572868
